TPU v7x, 256 devices: a whole 4x4x8 slice. The times are simulated.
256 devices in a mesh: dom: 16 (over x, y), slab: 16 (over z, core).
Axes of the slice: x: 4, y: 4, z: 8, core: 2. Of those that a mesh axis runs over, the one named last changes fastest.
Arguments:
- images: bfloat16 [4096, 8192], P(('dom', 'slab')), may hold values from -64 to 64
- defocus: bfloat16 [4096], P(('dom', 'slab')), may hold values from 20 to 60
- inv_noise: float32 [4096], replicated, may hold values from 0.01 to 0.04
- slices: bfloat16 [128, 8192], P('slab'), may hold values from -5 to 5
- lists: int32 [4096, 32], P(('dom', 'slab')), may hold values from 0 to 127, as said below
- counts: int32 [4096], P(('dom', 'slab')), may hold values from 0 to 32, as said below
Outputs:
- peak_weight: float32 [4096], P(('dom', 'slab'))
- data_sum: float32 [128, 8192], P('slab', 'dom')
- weight_sum: float32 [128, 4096], P('slab', 'dom')
Inputs may be any that keep to these rules, and one draw needn't show every extreme that they name: `lists`: the 32 entries of a row are different orientations. `counts`: 0 marks a particle left out of this pass; a particle that takes part has 2 or more significant orientations.
All inputs are finite; a program needn't handle non-finite values.
Results may differ from a plain program's by a relative error of at most 0.009.
Values may be sent and summed in bfloat16 or wider, within the bound.
No kernel may reach another device: no remote copies, remote signals or barrier semaphores. Data moves between devices by JAX's collectives and lax.ppermute only.
A program may use at most 128 MiB of HBM per device.

v0:
```python
import math

import jax
import jax.numpy as jnp
from jax import lax
from jax.sharding import PartitionSpec as P

SIDE = 64
COEF = 4096
TRANS = 25


SENTINEL = -1e30
HIGHEST = lax.Precision.HIGHEST


def frequency_grid():
    position = jnp.arange(COEF, dtype=jnp.int32)
    freq_x = (position // SIDE - SIDE // 2).astype(jnp.float32)
    freq_y = (position % SIDE - SIDE // 2).astype(jnp.float32)
    return (freq_x, freq_y)


def shift_tables(freq_x, freq_y):
    edge = math.isqrt(TRANS)
    half = edge // 2
    offsets = jnp.arange(TRANS, dtype=jnp.int32)
    shift_x = (offsets // edge - half).astype(jnp.float32)
    shift_y = (offsets % edge - half).astype(jnp.float32)
    angle = (
        2.0
        * jnp.pi
        * (shift_x[:, None] * freq_x[None, :] + shift_y[:, None] * freq_y[None, :])
        / SIDE
    )
    return (jnp.cos(angle), jnp.sin(angle))


def rotate_rows(values, cosine, sine):
    real_part = values[:, None, :COEF]
    imag_part = values[:, None, COEF:]
    turned = jnp.concatenate(
        (real_part * cosine - imag_part * sine, real_part * sine + imag_part * cosine), axis=-1
    )
    return turned.reshape(values.shape[0] * TRANS, 2 * COEF)


def significance(lists, counts, offset, number):
    orient_ids = offset + jnp.arange(number, dtype=jnp.int32)
    slot_live = jnp.arange(lists.shape[1], dtype=jnp.int32)[None, :] < counts[:, None]
    hits = (lists[:, :, None] == orient_ids[None, None, :]) & slot_live[:, :, None]
    return jnp.any(hits, axis=1)


def expectation(
    images,
    defocus,
    lists,
    counts,
    inv_noise,
    slices,
    offset,
    tile,
    reduce_highest,
    reduce_normalizer,
):
    row_count = images.shape[0]
    orient_count = slices.shape[0]
    freq_x, freq_y = frequency_grid()
    cosine, sine = shift_tables(freq_x, freq_y)
    radius = (freq_x * freq_x + freq_y * freq_y) / (SIDE * SIDE)
    ordering = jnp.argsort((counts <= 0).astype(jnp.int32), stable=True)
    sorted_images = jnp.take(images, ordering, axis=0)
    sorted_defocus = jnp.take(defocus, ordering, axis=0)
    sorted_lists = jnp.take(lists, ordering, axis=0)
    sorted_counts = jnp.take(counts, ordering, axis=0)
    alive = sorted_counts > 0
    live_tiles = (jnp.sum(alive.astype(jnp.int32)) + tile - 1) // tile
    ctf = -jnp.sin(jnp.pi * sorted_defocus.astype(jnp.float32)[:, None] * radius[None, :] + 0.1)
    real_part = sorted_images[:, :COEF].astype(jnp.float32)
    imag_part = sorted_images[:, COEF:].astype(jnp.float32)
    weighted = jnp.concatenate(
        (inv_noise * ctf * real_part, inv_noise * ctf * imag_part), axis=-1
    ).astype(jnp.bfloat16)
    image_half = jnp.concatenate((ctf * real_part, ctf * imag_part), axis=-1).astype(jnp.bfloat16)
    quad_half = -0.5 * inv_noise * ctf * ctf
    quadratic = jnp.concatenate((quad_half, quad_half), axis=-1).astype(jnp.bfloat16)
    slices_wide = slices.astype(jnp.float32)
    squares = (slices_wide * slices_wide).astype(jnp.bfloat16)
    energy = lax.dot_general(
        quadratic, squares, (((1,), (1,)), ((), ())), preferred_element_type=jnp.float32
    )
    mask = significance(sorted_lists, sorted_counts, offset, orient_count)

    def score_step(tile_step, buffer):
        rows_weighted = weighted.astype(jnp.float32)
        linear = lax.dot_general(
            rotate_rows(rows_weighted, cosine, sine),
            slices_wide,
            (((1,), (1,)), ((), ())),
            precision=HIGHEST,
        )
        linear = linear.reshape(tile, TRANS, orient_count)
        score = jnp.where(mask[:, None, :], linear + energy[:, None, :], SENTINEL)
        return score

    start_buffer = jnp.full((row_count, TRANS, orient_count), SENTINEL, jnp.float32)
    buffer = lax.fori_loop(0, live_tiles, score_step, start_buffer)
    highest = reduce_highest(jnp.max(buffer, axis=(1, 2)))
    highest = jnp.where(alive, highest, 0.0)
    expo = jnp.where(buffer > 0.5 * SENTINEL, jnp.exp(buffer - highest[:, None, None]), 0.0)
    normalizer = reduce_normalizer(jnp.sum(expo, axis=(1, 2)))
    normalizer = jnp.where(alive, normalizer, 1.0)
    posterior_half = (expo / normalizer[:, None, None]).astype(jnp.bfloat16)
    peak_sorted = jnp.where(alive, 1.0 / normalizer, 0.0)
    peak_values = jnp.zeros((row_count,), jnp.float32).at[ordering].set(peak_sorted)

    def sum_step(tile_step, total):
        return total + lax.dot_general(
            posterior_half.astype(jnp.float32).reshape(tile * TRANS, orient_count),
            rotate_rows(image_half.astype(jnp.float32), cosine, sine),
            (((0,), (0,)), ((), ())),
            precision=HIGHEST,
        )

    data_sum = lax.fori_loop(
        0, live_tiles, sum_step, jnp.zeros((orient_count, 2 * COEF), jnp.float32)
    )
    per_orient = jnp.sum(posterior_half.astype(jnp.float32), axis=1)
    ctf_half = (ctf * ctf).astype(jnp.bfloat16).astype(jnp.float32)
    weight_sum = lax.dot_general(per_orient, ctf_half, (((0,), (0,)), ((), ())), precision=HIGHEST)
    return (peak_values, data_sum, weight_sum)


def keep_values(values):
    return values


def shards(images, defocus, inv_noise, slices, lists, counts):
    whole_slices = lax.all_gather(slices, "slab", axis=0, tiled=True)
    peak_weight, data_sum, weight_sum = expectation(
        images, defocus, lists, counts, inv_noise, whole_slices, 0, 16, keep_values, keep_values
    )
    data_sum, weight_sum = (
        lax.psum_scatter(data_sum, "slab", scatter_dimension=0, tiled=True),
        lax.psum_scatter(weight_sum, "slab", scatter_dimension=0, tiled=True),
    )
    data_sum, weight_sum = (
        lax.psum_scatter(data_sum, "dom", scatter_dimension=1, tiled=True),
        lax.psum_scatter(weight_sum, "dom", scatter_dimension=1, tiled=True),
    )
    return (peak_weight, data_sum, weight_sum)


def solution(mesh):
    placed = (
        P(("dom", "slab"), None),
        P(("dom", "slab")),
        P(),
        P("slab", None),
        P(("dom", "slab"), None),
        P(("dom", "slab")),
    )
    return jax.shard_map(
        shards,
        mesh=mesh,
        in_specs=placed,
        out_specs=(P(("dom", "slab")), P("slab", "dom"), P("slab", "dom")),
        check_vma=False,
    )
```

profile of v0, /device:TPU:1, one launch (start us, length us, event | category | flops | bytes accessed | tf_op | source)
XLA Modules:
  0.0 366.1 jit_solution(13582859348225433491)
XLA Ops:
  8.6 1.2 sort.17
  9.9 1.3 gather_fusion
  11.2 1.3 gather_fusion.2
  14.0 1.3 gather_fusion.1
  17.1 1.8 fusion.25
  18.9 1.9 fusion.24
  20.9 7.0 %multiply_subtract_fusion.1 = (f32[16,25,4096]{2,1,0:T(8,128)}, f32[16,25,4096]{2,1,0:T(8,128)}) fusion(f32[25,4096]{1,0:T(8,128)S(1)} %get-tuple-element.288, f32[16,4096]{1,0:T(8,128)S(1)} %get-tuple-element.282, f32[25,4096]{1,0:T(8,128)S(1)} %get-tuple-element.287, f32[16,4096]{1,0:T(8,128)S(1)} %get-tuple-element.281), kind=kLoop, calls=%fused_computation.25 | loop fusion | flops 9830400 | bytes 14450688 | tf_op jit(solution)/shard_map/while/body/sub | solution.py:43
  27.9 25.5 %all-gather.2.cloned.1.call-done = bf16[128,8192]{1,0:T(8,128)(2,1)} async-done(((bf16[8,8192]{1,0:T(8,128)(2,1)}), bf16[128,8192]{1,0:T(8,128)(2,1)}) %all-gather.2.cloned.1.call-update) | async-done | bytes 2097168 | tf_op jit(solution)/shard_map/all_gather | solution.py:140
  53.5 2.2 fusion.21
  55.7 12.4 %fusion.17 = f32[16,25,128]{2,1,0:T(8,128)S(1)} fusion(f32[16,25,4096]{2,1,0:T(8,128)} %get-tuple-element.280, f32[16,25,4096]{2,1,0:T(8,128)} %get-tuple-element.279, bf16[128,8192]{1,0:T(8,128)(2,1)} %all-gather.2.cloned.1.call-done), kind=kOutput, calls=%fused_computation.20 | convolution fusion | flops 5036441600 | bytes 15409152 | tf_op jit(solution)/shard_map/while/body/dot_general | solution.py:97
  69.6 1.2 reduce_max.9
  70.7 1.3 fusion.37
  72.0 1.1 convert_reduce_fusion
  73.1 3.0 fusion.38
  76.2 2.2 broadcast_in_dim.94
  78.4 29.6 %while.26 = (s32[]{:T(128)}, f32[128,8192]{0,1:T(8,128)}, s32[]{:T(128)}, bf16[16,8192]{1,0:T(8,128)(2,1)S(1)}, bf16[16,25,128]{2,1,0:T(8,128)(2,1)S(1)}, /*inde...) while((s32[]{:T(128)}, f32[128,8192]{0,1:T(8,128)}, ...), condition=%wide.region_9.10_spmd.clone.clone.clone, body=%wide.region_8.9_spmd.clone.clone.clone.sunk | while | flops 5047730176 | bytes 37949740 | solution.py:126
  78.5 1.9 fusion.73
  80.4 7.0 %multiply_subtract_fusion.3 = (f32[16,25,4096]{2,1,0:T(8,128)}, f32[16,25,4096]{2,1,0:T(8,128)}) fusion(f32[25,4096]{1,0:T(8,128)S(1)} %get-tuple-element.396, f32[16,4096]{1,0:T(8,128)S(1)} %get-tuple-element.397, f32[25,4096]{1,0:T(8,128)S(1)} %get-tuple-element.398, f32[16,4096]{1,0:T(8,128)S(1)} %get-tuple-element.399), kind=kLoop, calls=%fused_computation.15.clone.1 | loop fusion | flops 9830400 | bytes 14450688 | tf_op jit(solution)/shard_map/while/body/sub | solution.py:43
  87.5 20.6 %fusion.75 = f32[128,8192]{0,1:T(8,128)} fusion(f32[128,8192]{0,1:T(8,128)} %get-tuple-element.434, bf16[16,25,128]{2,1,0:T(8,128)(2,1)S(1)} %get-tuple-element.447, f32[16,25,4096]{2,1,0:T(8,128)} %get-tuple-element.400, f32[16,25,4096]{2,1,0:T(8,128)} %get-tuple-element.401), kind=kOutput, calls=%fused_computation.13.clone.1 | convolution fusion | flops 5037490176 | bytes 21598208 | tf_op jit(solution)/shard_map/while/body/dot_general | solution.py:119
  108.0 5.6 %copy.11 = f32[128,8192]{1,0:T(8,128)} copy(f32[128,8192]{0,1:T(8,128)} %get-tuple-element.146) | data formatting | bytes 8388608 | tf_op jit(solution)/shard_map/while | solution.py:126
  113.8 17.7 %reduce-scatter.9.cloned.1.call-done = f32[8,4096]{1,0:T(8,128)} async-done(((f32[128,4096]{1,0:T(8,128)}), f32[8,4096]{1,0:T(8,128)}) %reduce-scatter.9.cloned.1.call-update) | async-done | bytes 131088 | tf_op jit(solution)/shard_map/reduce_scatter | solution.py:146
  131.5 64.5 %reduce-scatter.5.cloned.1.call-done = f32[8,8192]{1,0:T(8,128)} async-done(((f32[128,8192]{1,0:T(8,128)}), f32[8,8192]{1,0:T(8,128)}) %reduce-scatter.5.cloned.1.call-update) | async-done | bytes 262160 | tf_op jit(solution)/shard_map/reduce_scatter | solution.py:145
  197.2 80.5 %reduce-scatter.11.cloned.1.call-done = f32[8,256]{1,0:T(8,128)} async-done(((f32[8,4096]{1,0:T(8,128)}), f32[8,256]{1,0:T(8,128)}) %reduce-scatter.11.cloned.1.call-update) | async-done | bytes 8208 | tf_op jit(solution)/shard_map/reduce_scatter | solution.py:150
  277.6 82.0 %reduce-scatter.7.cloned.1.call-done = f32[8,512]{1,0:T(8,128)} async-done(((f32[8,8192]{1,0:T(8,128)}), f32[8,512]{1,0:T(8,128)}) %reduce-scatter.7.cloned.1.call-update) | async-done | bytes 16400 | tf_op jit(solution)/shard_map/reduce_scatter | solution.py:149
  (36 shorter events, 7.6 us)
Async XLA Ops:
  7.2 8.9 %copy-start = (bf16[16,8192]{1,0:T(8,128)(2,1)S(1)}, bf16[16,8192]{1,0:T(8,128)(2,1)}, u32[]{:S(2)}) copy-start(bf16[16,8192]{1,0:T(8,128)(2,1)} %param.10) | copy-start | bytes 786436
  7.2 46.3 %all-gather.2.cloned.1.call-start = ((), (), s32[]{:S(2)}) async-start(), calls=%async_computation.4 | async-start | bytes 2228224 | tf_op jit(solution)/shard_map/all_gather | solution.py:140
  7.9 123.5 %reduce-scatter.9.cloned.1.call-start = ((), (), s32[]{:S(2)}) async-start(), calls=%async_computation.7 | async-start | bytes 2228224 | tf_op jit(solution)/shard_map/reduce_scatter | solution.py:146
  76.2 119.9 %reduce-scatter.5.cloned.1.call-start = ((), (), s32[]{:S(2)}) async-start(), calls=%async_computation.5 | async-start | bytes 4456448 | tf_op jit(solution)/shard_map/reduce_scatter | solution.py:145
  113.7 163.9 %reduce-scatter.11.cloned.1.call-start = ((), (), s32[]{:S(2)}) async-start(), calls=%async_computation.8 | async-start | bytes 139264 | tf_op jit(solution)/shard_map/reduce_scatter | solution.py:150
  131.5 228.2 %reduce-scatter.7.cloned.1.call-start = ((), (), s32[]{:S(2)}) async-start(), calls=%async_computation.6 | async-start | bytes 278528 | tf_op jit(solution)/shard_map/reduce_scatter | solution.py:149
Sparse Core Ops, SparseCore 0:
  9.8 43.5 all-gather.1
  76.3 55.0 reduce-scatter.8
  134.0 62.0 reduce-scatter.4
  199.9 77.6 reduce-scatter.10
  281.5 78.0 reduce-scatter.6
where the time goes:
time: 367 us; the launch traced here: 366 us
  waiting for transfers between devices  271 us (74%)
  matrix products  38.3 us (10%)
  other arithmetic  27.8 us (8%)
  between operations  14.6 us (4%)
  local copies, waits for them, and re-layouts  14.4 us (4%)
    reduce_scatter x1, waiting for transfers between devices, shards(): lax.psum_scatter(data_sum, 'dom', scatter_dimension=1, tiled=True)  82 us
    reduce_scatter x1, waiting for transfers between devices, shards(): lax.psum_scatter(weight_sum, 'dom', scatter_dimension=1, tiled=True)  80.5 us
    reduce_scatter x1, waiting for transfers between devices, shards(): lax.psum_scatter(data_sum, 'slab', scatter_dimension=0, tiled=True)  64.5 us
    all_gather x1, waiting for transfers between devices, shards(): whole_slices = lax.all_gather(slices, 'slab', axis=0, tiled=True)  25.5 us
    dot_general x1, matrix products, sum_step(): lax.dot_general(posterior_half.astype(jnp.float32).reshape(tile * TRANS,...  20.6 us
    reduce_scatter x1, waiting for transfers between devices, shards(): lax.psum_scatter(weight_sum, 'slab', scatter_dimension=0, tiled=True)  17.7 us
    sub x2, other arithmetic, rotate_rows(): real_part * cosine - imag_part * sine  14.1 us
    dot_general x1, matrix products, score_step(): lax.dot_general(rotate_rows(rows_weighted, cosine, sine), slices_wide, ((...  12.4 us
  transfers between devices with their start and end apart: 5, of which 5 were waited for; matrix products, arithmetic and copies ran while one was open for 16% of the time, Pallas kernels for 0%

commit v1 on v0

v1 whole, which is shorter than its diff:
```python
import math

import numpy as np
import jax
import jax.numpy as jnp
from jax import lax
from jax.sharding import Mesh
from jax.sharding import PartitionSpec as P

SIDE = 64
COEF = 4096
PIX = 2 * COEF
TRANS = 25

SENTINEL = -1e30
HIGHEST = lax.Precision.HIGHEST


def _tables():
    position = np.arange(COEF)
    freq_x = (position // SIDE - SIDE // 2).astype(np.float64)
    freq_y = (position % SIDE - SIDE // 2).astype(np.float64)
    edge = math.isqrt(TRANS)
    half = edge // 2
    offsets = np.arange(TRANS)
    shift_x = (offsets // edge - half).astype(np.float64)
    shift_y = (offsets % edge - half).astype(np.float64)
    angle = 2.0 * np.pi * (shift_x[:, None] * freq_x[None, :] + shift_y[:, None] * freq_y[None, :]) / SIDE
    radius = (freq_x * freq_x + freq_y * freq_y) / (SIDE * SIDE)
    return (
        np.cos(angle).astype(np.float32),
        np.sin(angle).astype(np.float32),
        radius.astype(np.float32),
    )


COSINE, SINE, RADIUS = _tables()


def split3(values):
    first = values.astype(jnp.bfloat16)
    rest = values - first.astype(jnp.float32)
    second = rest.astype(jnp.bfloat16)
    third = (rest - second.astype(jnp.float32)).astype(jnp.bfloat16)
    return first, second, third


def shards(images, defocus, inv_noise, slices, lists, counts):
    rows = images.shape[0]
    own_orients = slices.shape[0]
    orient_total = own_orients * lax.axis_size("zz") * lax.axis_size("cc")
    pad = (-(orient_total + 2)) % 128
    zz = lax.axis_index("zz")
    cc = lax.axis_index("cc")
    group = lax.axis_size("zz")

    orient_ids = jnp.arange(orient_total, dtype=jnp.int32)
    slot_live = jnp.arange(lists.shape[1], dtype=jnp.int32)[None, :] < counts[:, None]
    hits = (lists[:, :, None] == orient_ids[None, None, :]) & slot_live[:, :, None]
    mask_all = jnp.any(hits, axis=1)
    alive = counts > 0
    extra = jnp.concatenate(
        (
            mask_all.astype(jnp.bfloat16),
            alive.astype(jnp.bfloat16)[:, None],
            defocus[:, None],
            jnp.zeros((rows, pad), jnp.bfloat16),
        ),
        axis=1,
    )
    packed = jnp.concatenate((images, extra), axis=1)
    gathered = lax.all_gather(packed, "zz", axis=0, tiled=True)
    local_slices = lax.all_gather(slices, "cc", axis=0, tiled=True)
    count = gathered.shape[0]
    chip_orients = local_slices.shape[0]

    g_images = gathered[:, :PIX]
    g_mask_all = gathered[:, PIX : PIX + orient_total]
    g_alive = gathered[:, PIX + orient_total] > 0.5
    g_defocus = gathered[:, PIX + orient_total + 1].astype(jnp.float32)
    mask = lax.dynamic_slice_in_dim(g_mask_all, zz * chip_orients, chip_orients, 1) > 0.5

    cosine = jnp.asarray(COSINE)
    sine = jnp.asarray(SINE)
    radius = jnp.asarray(RADIUS)
    ctf = -jnp.sin(jnp.pi * g_defocus[:, None] * radius[None, :] + 0.1)
    real_part = g_images[:, :COEF].astype(jnp.float32)
    imag_part = g_images[:, COEF:].astype(jnp.float32)
    weighted = jnp.concatenate(
        (inv_noise * ctf * real_part, inv_noise * ctf * imag_part), axis=-1
    ).astype(jnp.bfloat16)
    image_half = jnp.concatenate((ctf * real_part, ctf * imag_part), axis=-1).astype(jnp.bfloat16)
    quad_half = (-0.5 * inv_noise * ctf * ctf).astype(jnp.bfloat16)
    ctf_half = (ctf * ctf).astype(jnp.bfloat16)

    slices_wide = local_slices.astype(jnp.float32)
    squares = (slices_wide * slices_wide).astype(jnp.bfloat16)
    energy = lax.dot_general(
        quad_half, squares[:, :COEF], (((1,), (1,)), ((), ())), preferred_element_type=jnp.float32
    ) + lax.dot_general(
        quad_half, squares[:, COEF:], (((1,), (1,)), ((), ())), preferred_element_type=jnp.float32
    )

    s_real = slices_wide[None, :, :COEF]
    s_imag = slices_wide[None, :, COEF:]
    c_t = cosine[:, None, :]
    s_t = sine[:, None, :]
    turned = jnp.concatenate((c_t * s_real + s_t * s_imag, c_t * s_imag - s_t * s_real), axis=-1)
    turned = turned.reshape(TRANS * chip_orients, PIX)
    parts = jnp.concatenate(split3(turned), axis=0)
    linear3 = lax.dot_general(
        weighted, parts, (((1,), (1,)), ((), ())), preferred_element_type=jnp.float32
    )
    block = TRANS * chip_orients
    linear = linear3[:, :block] + linear3[:, block : 2 * block] + linear3[:, 2 * block :]
    linear = linear.reshape(count, TRANS, chip_orients)
    score = jnp.where(mask[:, None, :], linear + energy[:, None, :], SENTINEL)

    local_max = jnp.max(score, axis=(1, 2))
    local_sum = jnp.sum(
        jnp.where(mask[:, None, :], jnp.exp(score - local_max[:, None, None]), 0.0), axis=(1, 2)
    )
    stats = lax.all_gather(jnp.stack((local_max, local_sum)), "zz", axis=0)
    highest = jnp.max(stats[:, 0], axis=0)
    normalizer = jnp.sum(stats[:, 1] * jnp.exp(stats[:, 0] - highest[None, :]), axis=0)
    highest = jnp.where(g_alive, highest, 0.0)
    normalizer = jnp.where(g_alive, normalizer, 1.0)
    expo = jnp.where(mask[:, None, :], jnp.exp(score - highest[:, None, None]), 0.0)
    posterior = (expo / normalizer[:, None, None]).astype(jnp.bfloat16)
    posterior = jnp.where(g_alive[:, None, None], posterior, jnp.zeros_like(posterior))
    peak_all = jnp.where(g_alive, 1.0 / normalizer, 0.0)
    peak_weight = lax.dynamic_slice_in_dim(peak_all, zz * rows, rows, 0)

    flat_post = posterior.reshape(count, block)
    accum = lax.dot_general(
        flat_post, image_half, (((0,), (0,)), ((), ())), preferred_element_type=jnp.float32
    ).reshape(TRANS, chip_orients, PIX)
    a_real = accum[:, :, :COEF]
    a_imag = accum[:, :, COEF:]
    data_real = jnp.sum(c_t * a_real - s_t * a_imag, axis=0)
    data_imag = jnp.sum(s_t * a_real + c_t * a_imag, axis=0)
    data = jnp.concatenate((data_real, data_imag), axis=-1)

    per_orient = jnp.sum(posterior.astype(jnp.float32), axis=1)
    weight = lax.dot_general(
        per_orient, ctf_half.astype(jnp.float32), (((0,), (0,)), ((), ())), precision=HIGHEST
    )

    doms = lax.axis_size("dom")
    halves = lax.axis_size("cc")
    data_cols = PIX // doms
    weight_cols = COEF // doms
    data_b = data.reshape(halves, own_orients, doms, data_cols).transpose(0, 2, 1, 3)
    weight_b = weight.reshape(halves, own_orients, doms, weight_cols).transpose(0, 2, 1, 3)
    both = jnp.concatenate((data_b, weight_b), axis=-1).reshape(
        halves * doms * own_orients, data_cols + weight_cols
    )
    reduced = lax.psum_scatter(both, ("cc", "dom"), scatter_dimension=0, tiled=True)
    data_out = reduced[:, :data_cols]
    weight_out = reduced[:, data_cols:]
    return (peak_weight, data_out, weight_out)


def solution(mesh):
    doms = mesh.shape["dom"]
    slabs = mesh.shape["slab"]
    split = Mesh(mesh.devices.reshape(doms, slabs // 2, 2), ("dom", "zz", "cc"))
    rowwise = ("dom", "zz", "cc")
    placed = (
        P(rowwise, None),
        P(rowwise),
        P(),
        P(("zz", "cc"), None),
        P(rowwise, None),
        P(rowwise),
    )
    return jax.shard_map(
        shards,
        mesh=split,
        in_specs=placed,
        out_specs=(P(rowwise), P(("zz", "cc"), "dom"), P(("zz", "cc"), "dom")),
        check_vma=False,
    )
```

time: 367 us -> 216 us (0.59)
  waiting for transfers between devices: 271 us -> 113 us
  blocking collectives: 0 us -> 16.6 us
  local copies, waits for them, and re-layouts: 14.4 us -> 6.03 us
    reduce_scatter x4 -> x1, waiting for transfers between devices: 245 us -> 90 us  [shards(): lax.psum_scatter(both, ('cc', 'dom'), scatter_dimension=0, tiled=True)]
    all_gather x0 -> x2, blocking collectives: none -> 16.6 us  [the longest x1 11.6 us: shards(): stats = lax.all_gather(jnp.stack((local_max, local_sum)), 'zz', axis=0)]
    sub x2 -> x0, other arithmetic: 14.1 us -> none  [rotate_rows(): real_part * cosine - imag_part * sine]
    convert_element_type x4, other arithmetic: 0.74 us -> 8.93 us  [the longest x1 5.61 us: split3(): second = rest.astype(jnp.bfloat16)]
    another operation x1, other arithmetic: 1.75 us -> 9.27 us
    while x1 -> x0, local copies, waits for them, and re-layouts: 5.65 us -> none  [expectation(): lax.fori_loop(0, live_tiles, sum_step, jnp.zeros((orient_count, 2 * COEF)...]
    gather x4 -> x0, local copies, waits for them, and re-layouts: 4.6 us -> none  [the longest x1 1.32 us: expectation(): sorted_defocus = jnp.take(defocus, ordering, axis=0)]
    cos x2 -> x0, other arithmetic: 3.87 us -> none  [shift_tables(): return (jnp.cos(angle), jnp.sin(angle))]
  transfers between devices with their start and end apart: 5 -> 2, of which waited for: 5 -> 2; matrix products, arithmetic and copies ran while one was open for 16% -> 6% of each run, Pallas kernels for 0% -> 0%
where the time goes in v1:
time: 216 us; the launch traced here: 215 us
  waiting for transfers between devices  113 us (52%)
  matrix products  36 us (17%)
  other arithmetic  29.3 us (14%)
  blocking collectives  16.6 us (8%)
  between operations  14.2 us (7%)
  local copies, waits for them, and re-layouts  6.03 us (3%)
    reduce_scatter x1, waiting for transfers between devices, shards(): lax.psum_scatter(both, ('cc', 'dom'), scatter_dimension=0, tiled=True)  90 us
    all_gather x1, waiting for transfers between devices, shards(): gathered = lax.all_gather(packed, 'zz', axis=0, tiled=True)  23 us
    all_gather x1, blocking collectives, shards(): stats = lax.all_gather(jnp.stack((local_max, local_sum)), 'zz', axis=0)  11.6 us
    dot_general x1, matrix products, shards(): lax.dot_general(weighted, parts, (((1,), (1,)), ((), ())), preferred_elem...  9.7 us
    dot_general x1, matrix products, shards(): lax.dot_general(per_orient, ctf_half.astype(jnp.float32), (((0,), (0,)),...  9.44 us
    another operation x1, other arithmetic  9.27 us
    dot_general x1, matrix products, shards(): lax.dot_general(quad_half, squares[:, COEF:], (((1,), (1,)), ((), ())), p...  7.62 us
    dot_general x1, matrix products, shards(): lax.dot_general(quad_half, squares[:, :COEF], (((1,), (1,)), ((), ())), p...  7.43 us
  transfers between devices with their start and end apart: 2, of which 2 were waited for; matrix products, arithmetic and copies ran while one was open for 6% of the time, Pallas kernels for 0%

profile of v1, /device:TPU:1, one launch (start us, length us, event | category | flops | bytes accessed | tf_op | source)
XLA Modules:
  0.0 215.3 jit_solution(8718423619522921460)
XLA Ops:
  7.2 0.7 iota_compare_fusion.1
  8.6 0.9 fusion.29
  9.6 0.7 copy.33
  10.4 1.7 concatenate.24
  12.2 5.0 %all_gather.13 = bf16[16,8192]{1,0:T(8,128)(2,1)S(1)} all-gather(bf16[8,8192]{1,0:T(8,128)(2,1)} %param.12), channel_id=1, replica_groups=mesh['dom'=16,'zz'=8,'cc'=2] {'cc'}, dimensions={0}, use_global_device_ids=true | all-gather | bytes 393216 | tf_op jit(solution)/shard_map/all_gather | solution.py:73
  17.3 0.7 broadcast_multiply_fusion
  18.0 2.9 %multiply_add_fusion = (f32[25,16,4096]{2,1,0:T(8,128)S(1)}, f32[25,16,4096]{2,1,0:T(8,128)S(1)}) fusion(f32[16,4096]{1,0:T(8,128)S(1)} %get-tuple-element.18, f32[25,4096]{1,0:T(8,128)} %constant.17.clone, f32[16,4096]{1,0:T(8,128)S(1)} %get-tuple-element.17, f32[25,4096]{1,0:T(8,128)} %constant.16.clone), kind=kLoop, calls=%fused_computation.14 | loop fusion | flops 9830400 | bytes 14450688 | tf_op jit(solution)/shard_map/add | solution.py:108
  20.9 3.3 %fusion.6 = bf16[400,8192]{1,0:T(8,128)(2,1)} fusion(f32[400,4096]{1,0:T(8,128)S(1)} %bitcast.71, f32[400,4096]{1,0:T(8,128)S(1)} %bitcast.69), kind=kLoop, calls=%fused_computation.9 | loop fusion | flops 13107200 | bytes 19660800 | tf_op jit(solution)/shard_map/convert_element_type | solution.py:41
  24.2 5.6 %fusion.7 = (bf16[400,8192]{1,0:T(8,128)(2,1)}, bf16[400,8192]{1,0:T(8,128)(2,1)}) fusion(f32[400,4096]{1,0:T(8,128)S(1)} %bitcast.72, f32[400,4096]{1,0:T(8,128)S(1)} %bitcast.70), kind=kLoop, calls=%fused_computation.10 | loop fusion | flops 26214400 | bytes 26214400 | tf_op jit(solution)/shard_map/convert_element_type | solution.py:43
  29.9 23.0 %all-gather.4.cloned.1.call-done = bf16[128,8448]{1,0:T(8,128)(2,1)} async-done(((bf16[16,8448]{1,0:T(8,128)(2,1)}), bf16[128,8448]{1,0:T(8,128)(2,1)}) %all-gather.4.cloned.1.call-update) | async-done | bytes 2162704 | tf_op jit(solution)/shard_map/all_gather | solution.py:72
  52.9 0.9 multiply_reduce_fusion
  53.9 7.4 %fusion.26 = f32[128,16]{0,1:T(8,128)S(1)} fusion(f32[4096]{0:T(1024)S(1)} %broadcast_multiply_fusion, f32[4096]{0:T(1024)S(1)} %copy-done.3, f32[128]{0:T(128)S(1)} %multiply_reduce_fusion, bf16[16,8192]{1,0:T(8,128)(2,1)S(1)} %multiply_convert_fusion.1), kind=kOutput, calls=%fused_computation.41 | convolution fusion | flops 19922944 | bytes 172544 | tf_op jit(solution)/shard_map/dot_general | solution.py:98
  61.3 7.6 %convolution_add_fusion = f32[128,16]{0,1:T(8,128)S(1)} fusion(f32[128,16]{0,1:T(8,128)S(1)} %fusion.26, f32[4096]{0:T(1024)S(1)} %broadcast_multiply_fusion, f32[4096]{0:T(1024)S(1)} %copy-done.3, f32[128]{0:T(128)S(1)} %multiply_reduce_fusion, bf16[16,8192]{1,0:T(8,128)(2,1)S(1)} %multiply_convert_fusion.1), kind=kOutput, calls=%fused_computation.36 | convolution fusion | flops 19924992 | bytes 180736 | tf_op jit(solution)/shard_map/dot_general | solution.py:100
  69.1 9.3 %fusion.9 = (bf16[128,4096]{1,0:T(8,128)(2,1)S(1)}, bf16[128,4096]{1,0:T(8,128)(2,1)S(1)}, bf16[128,4096]{1,0:T(8,128)(2,1)S(1)}, bf16[128,4096]{1,0:T(8,128)(2,1)S(1)}) fusion(f32[4096]{0:T(1024)S(1)} %copy-done.3, f32[128]{0:T(128)S(1)} %multiply_reduce_fusion, bf16[128,8448]{1,0:T(8,128)(2,1)} %all-gather.4.cloned.1.call-done, f32[4096]{0:T(1024)S(1)} %copy-done.2), kind=kLoop, calls=%fused_computation.21 | loop fusion | flops 7340032 | bytes 6324736 | tf_op jit(solution)/shard_map/convert.1
  78.4 9.7 %fusion = f32[128,1200]{0,1:T(8,128)S(1)} fusion(bf16[400,8192]{1,0:T(8,128)(2,1)} %get-tuple-element.8, bf16[400,8192]{1,0:T(8,128)(2,1)} %get-tuple-element.7, bf16[400,8192]{1,0:T(8,128)(2,1)} %fusion.6, bf16[128,4096]{1,0:T(8,128)(2,1)S(1)} %get-tuple-element.13, bf16[128,4096]{1,0:T(8,128)(2,1)S(1)} %get-tuple-element.14), kind=kOutput, calls=%fused_computation | convolution fusion | flops 2579759104 | bytes 22372352 | tf_op jit(solution)/shard_map/dot_general | solution.py:111
  88.3 11.6 %all-gather.1 = f32[8,2,128]{2,1,0:T(2,128)S(1)} all-gather(f32[1,2,128]{2,1,0:T(2,128)S(1)} %maximum_bitcast_fusion.2), channel_id=2, replica_groups=mesh['dom'=16,'zz'=8,'cc'=2] {'zz'}, dimensions={0}, use_global_device_ids=true | all-gather | bytes 9216 | tf_op jit(solution)/shard_map/all_gather | solution.py:123
  99.9 0.9 compare_reduce_fusion
  100.9 1.9 fusion.16
  102.8 2.0 subtract_reduce_fusion
  104.8 9.4 %convolution_bitcast_fusion = f32[2,16,8,256]{3,2,1,0:T(8,128)S(1)} fusion(f32[16,256]{1,0:T(8,128)S(1)} %copy-done.4, f32[128]{0:T(128)S(1)} %multiply_reduce_fusion, f32[128,16]{0,1:T(8,128)S(1)} %convert_reduce_fusion), kind=kOutput, calls=%fused_computation.35 | convolution fusion | flops 102760448 | bytes 287232 | tf_op jit(solution)/shard_map/dot_general | solution.py:145
  114.3 0.9 pad_maximum_fusion.1
  115.8 90.0 %reduce-scatter.2.cloned.1.call-done = f32[8,768]{1,0:T(8,128)} async-done(((f32[256,768]{1,0:T(8,128)}), f32[8,768]{1,0:T(8,128)}) %reduce-scatter.2.cloned.1.call-update) | async-done | bytes 24592 | tf_op jit(solution)/shard_map/reduce_scatter | solution.py:158
  205.8 1.3 slice.92
  207.1 1.3 slice.93
  (36 shorter events, 2.2 us)
Async XLA Ops:
  7.2 45.7 %all-gather.4.cloned.1.call-start = ((), (), s32[]{:S(2)}) async-start(), calls=%async_computation.1 | async-start | bytes 2433024 | tf_op jit(solution)/shard_map/all_gather | solution.py:72
  12.1 193.7 %reduce-scatter.2.cloned.1.call-start = ((), (), s32[]{:S(2)}) async-start(), calls=%async_computation.2 | async-start | bytes 811008 | tf_op jit(solution)/shard_map/reduce_scatter | solution.py:158
  24.2 29.6 %copy-start.3 = (f32[4096]{0:T(1024)S(1)}, f32[4096]{0:T(1024)}, u32[]{:S(2)}) copy-start(f32[4096]{0:T(1024)} %constant.44.clone) | copy-start | bytes 49156
  29.8 39.3 %copy-start.2 = (f32[4096]{0:T(1024)S(1)}, f32[4096]{0:T(1024)}, u32[]{:S(2)}) copy-start(f32[4096]{0:T(1024)} %param.11) | copy-start | bytes 49156
  52.9 16.0 %slice-start = ((bf16[128,8448]{1,0:T(8,128)(2,1)}), bf16[128,128]{1,0:T(8,128)(2,1)S(1)}, s32[]{:S(2)}) async-start(bf16[128,8448]{1,0:T(8,128)(2,1)} %all-gather.4.cloned.1.call-done), calls=%async_computation.3 | async-start | bytes 65536 | tf_op jit(solution)/shard_map/slice | solution.py:78
  100.8 1.9 copy-start
  100.8 1.9 copy-start.1
  102.7 2.1 copy-start.4
Sparse Core Ops, SparseCore 0:
  12.3 40.6 all-gather.3
  115.4 90.4 reduce-scatter.1

commit v2 on v1

--- a/solution.py
+++ b/solution.py
@@ -45,6 +45,25 @@
     return first, second, third
 
 
+def ring_gather(values, axis, size):
+    ahead = values
+    behind = values
+    later = []
+    sooner = [values]
+    for step in range(size // 2):
+        ahead = lax.ppermute(ahead, axis, [(i, (i + 1) % size) for i in range(size)])
+        later.append(ahead)
+        if step < (size - 1) // 2:
+            behind = lax.ppermute(behind, axis, [(i, (i - 1) % size) for i in range(size)])
+            sooner.append(behind)
+    return jnp.concatenate(sooner + later[::-1], axis=0)
+
+
+def exchange(values, axis, size):
+    spread = jnp.broadcast_to(values[None], (size,) + values.shape)
+    return lax.all_to_all(spread, axis, 0, 0, tiled=True)
+
+
 def shards(images, defocus, inv_noise, slices, lists, counts):
     rows = images.shape[0]
     own_orients = slices.shape[0]
@@ -52,7 +71,6 @@
     pad = (-(orient_total + 2)) % 128
     zz = lax.axis_index("zz")
     cc = lax.axis_index("cc")
-    group = lax.axis_size("zz")
 
     orient_ids = jnp.arange(orient_total, dtype=jnp.int32)
     slot_live = jnp.arange(lists.shape[1], dtype=jnp.int32)[None, :] < counts[:, None]
@@ -69,7 +87,8 @@
         axis=1,
     )
     packed = jnp.concatenate((images, extra), axis=1)
-    gathered = lax.all_gather(packed, "zz", axis=0, tiled=True)
+    group = lax.axis_size("zz")
+    gathered = ring_gather(packed, "zz", group)
     local_slices = lax.all_gather(slices, "cc", axis=0, tiled=True)
     count = gathered.shape[0]
     chip_orients = local_slices.shape[0]
@@ -92,6 +111,9 @@
     image_half = jnp.concatenate((ctf * real_part, ctf * imag_part), axis=-1).astype(jnp.bfloat16)
     quad_half = (-0.5 * inv_noise * ctf * ctf).astype(jnp.bfloat16)
     ctf_half = (ctf * ctf).astype(jnp.bfloat16)
+    weighted, image_half, quad_half, ctf_half = lax.optimization_barrier(
+        (weighted, image_half, quad_half, ctf_half)
+    )
 
     slices_wide = local_slices.astype(jnp.float32)
     squares = (slices_wide * slices_wide).astype(jnp.bfloat16)
@@ -120,31 +142,34 @@
     local_sum = jnp.sum(
         jnp.where(mask[:, None, :], jnp.exp(score - local_max[:, None, None]), 0.0), axis=(1, 2)
     )
-    stats = lax.all_gather(jnp.stack((local_max, local_sum)), "zz", axis=0)
-    highest = jnp.max(stats[:, 0], axis=0)
-    normalizer = jnp.sum(stats[:, 1] * jnp.exp(stats[:, 0] - highest[None, :]), axis=0)
+    shift = zz * rows
+    stats = jnp.roll(jnp.stack((local_max, local_sum)), shift, axis=1)
+    stats = exchange(stats, "zz", group)
+    highest = jnp.roll(jnp.max(stats[:, 0], axis=0), -shift)
+    normalizer = jnp.sum(stats[:, 1] * jnp.exp(stats[:, 0] - jnp.max(stats[:, 0], axis=0)[None, :]), axis=0)
+    normalizer = jnp.roll(normalizer, -shift)
     highest = jnp.where(g_alive, highest, 0.0)
     normalizer = jnp.where(g_alive, normalizer, 1.0)
     expo = jnp.where(mask[:, None, :], jnp.exp(score - highest[:, None, None]), 0.0)
     posterior = (expo / normalizer[:, None, None]).astype(jnp.bfloat16)
     posterior = jnp.where(g_alive[:, None, None], posterior, jnp.zeros_like(posterior))
     peak_all = jnp.where(g_alive, 1.0 / normalizer, 0.0)
-    peak_weight = lax.dynamic_slice_in_dim(peak_all, zz * rows, rows, 0)
+    peak_weight = peak_all[:rows]
 
     flat_post = posterior.reshape(count, block)
     accum = lax.dot_general(
-        flat_post, image_half, (((0,), (0,)), ((), ())), preferred_element_type=jnp.float32
-    ).reshape(TRANS, chip_orients, PIX)
+        flat_post,
+        jnp.concatenate((image_half, ctf_half), axis=1),
+        (((0,), (0,)), ((), ())),
+        preferred_element_type=jnp.float32,
+    ).reshape(TRANS, chip_orients, PIX + COEF)
+    weight = jnp.sum(accum[:, :, PIX:], axis=0)
     a_real = accum[:, :, :COEF]
-    a_imag = accum[:, :, COEF:]
+    a_imag = accum[:, :, COEF:PIX]
     data_real = jnp.sum(c_t * a_real - s_t * a_imag, axis=0)
     data_imag = jnp.sum(s_t * a_real + c_t * a_imag, axis=0)
     data = jnp.concatenate((data_real, data_imag), axis=-1)
 
-    per_orient = jnp.sum(posterior.astype(jnp.float32), axis=1)
-    weight = lax.dot_general(
-        per_orient, ctf_half.astype(jnp.float32), (((0,), (0,)), ((), ())), precision=HIGHEST
-    )
 
     doms = lax.axis_size("dom")
     halves = lax.axis_size("cc")
@@ -155,7 +180,9 @@
     both = jnp.concatenate((data_b, weight_b), axis=-1).reshape(
         halves * doms * own_orients, data_cols + weight_cols
     )
-    reduced = lax.psum_scatter(both, ("cc", "dom"), scatter_dimension=0, tiled=True)
+    pieces = halves * doms
+    both = both.reshape(pieces, own_orients, data_cols + weight_cols)
+    reduced = jnp.sum(lax.all_to_all(both, ("cc", "dom"), 0, 0, tiled=True), axis=0)
     data_out = reduced[:, :data_cols]
     weight_out = reduced[:, data_cols:]
     return (peak_weight, data_out, weight_out)

time: 216 us -> 152 us (0.70)
  waiting for transfers between devices: 113 us -> 15.2 us
  local copies, waits for them, and re-layouts: 6.03 us -> 48.2 us
  matrix products: 36 us -> 13.2 us
  starting transfers between devices: 0.08 us -> 15.8 us
  between operations: 14.2 us -> 0.94 us
  blocking collectives: 16.6 us -> 28.1 us
    reduce_scatter x1 -> x0, waiting for transfers between devices: 90 us -> none  [shards(): lax.psum_scatter(both, ('cc', 'dom'), scatter_dimension=0, tiled=True)]
    all_to_all x0 -> x1, blocking collectives: none -> 25.6 us  [shards(): lax.all_to_all(both, ('cc', 'dom'), 0, 0, tiled=True)]
    all_gather x1 -> x0, waiting for transfers between devices: 23 us -> none  [shards(): gathered = lax.all_gather(packed, 'zz', axis=0, tiled=True)]
    concatenate x0 -> x1, local copies, waits for them, and re-layouts: none -> 16.4 us  [ring_gather(): return jnp.concatenate(sooner + later[::-1], axis=0)]
    ppermute x0 -> x7, local copies, waits for them, and re-layouts: none -> 16.2 us  [the longest x4 9.08 us: ring_gather(): lax.ppermute(ahead, axis, [(i, (i + 1) % size) for i in range(size)])]
    ppermute x0 -> x7, starting transfers between devices: none -> 11.9 us  [the longest x3 11.8 us: ring_gather(): lax.ppermute(behind, axis, [(i, (i - 1) % size) for i in range(size)])]
    all_gather x1 -> x0, blocking collectives: 11.6 us -> none  [shards(): stats = lax.all_gather(jnp.stack((local_max, local_sum)), 'zz', axis=0)]
    convert_element_type x0 -> x1, other arithmetic: none -> 10.3 us  [shards(): ctf_half = (ctf * ctf).astype(jnp.bfloat16)]
  transfers between devices with their start and end apart: 2 -> 8, of which waited for: 2 -> 3; matrix products, arithmetic and copies ran while one was open for 6% -> 16% of each run, Pallas kernels for 0% -> 0%
where the time goes in v2:
time: 152 us; the launch traced here: 151 us
  local copies, waits for them, and re-layouts  48.2 us (32%)
  other arithmetic  29.8 us (20%)
  blocking collectives  28.1 us (18%)
  starting transfers between devices  15.8 us (10%)
  waiting for transfers between devices  15.2 us (10%)
  matrix products  13.2 us (9%)
    all_to_all x1, blocking collectives, shards(): lax.all_to_all(both, ('cc', 'dom'), 0, 0, tiled=True)  25.6 us
    concatenate x1, local copies, waits for them, and re-layouts, ring_gather(): return jnp.concatenate(sooner + later[::-1], axis=0)  16.4 us
    ppermute x3, starting transfers between devices, ring_gather(): lax.ppermute(behind, axis, [(i, (i - 1) % size) for i in range(size)])  11.8 us
    convert_element_type x1, other arithmetic, shards(): ctf_half = (ctf * ctf).astype(jnp.bfloat16)  10.3 us
    concatenate x2, local copies, waits for them, and re-layouts, shards(): packed = jnp.concatenate((images, extra), axis=1)  10.1 us
    ppermute x4, local copies, waits for them, and re-layouts, ring_gather(): lax.ppermute(ahead, axis, [(i, (i + 1) % size) for i in range(size)])  9.08 us
    ppermute x4, waiting for transfers between devices, ring_gather(): lax.ppermute(ahead, axis, [(i, (i + 1) % size) for i in range(size)])  8.63 us
    dot_general x1, matrix products, shards(): lax.dot_general(weighted, parts, (((1,), (1,)), ((), ())), preferred_elem...  8.33 us
  transfers between devices with their start and end apart: 8, of which 3 were waited for; matrix products, arithmetic and copies ran while one was open for 16% of the time, Pallas kernels for 0%

profile of v2, /device:TPU:1, one launch (start us, length us, event | category | flops | bytes accessed | tf_op | source)
XLA Modules:
  0.0 151.3 jit_solution(17556624647020679881)
XLA Ops:
  2.2 2.6 %copy.46 = bf16[16,8192]{0,1:T(8,128)(2,1)} copy(bf16[16,8192]{1,0:T(8,128)(2,1)} %param.11) | data formatting | bytes 524288 | tf_op args[0]
  5.8 8.6 %concatenate.37 = bf16[16,8448]{0,1:T(8,128)(2,1)S(1)} concatenate(bf16[16,8192]{0,1:T(8,128)(2,1)} %copy.46, bf16[16,128]{0,1:T(8,128)(2,1)S(1)} %copy.47, bf16[16,1]{0,1:T(2,128)(2,1)S(1)} %fusion.31, bf16[16,1]{0,1:T(2,128)(2,1)} %bitcast.74, bf16[16,126]{0,1:T(8,128)(2,1)S(1)} %broadcast_in_dim.85), dimensions={1} | concatenate | bytes 540672 | tf_op jit(solution)/shard_map/concatenate | solution.py:89
  15.9 6.4 %collective-permute-start = (bf16[16,8448]{1,0:T(8,128)(2,1)}, bf16[16,8448]{1,0:T(8,128)(2,1)S(1)}, u32[]{:S(2)}, u32[]{:S(2)}) collective-permute-start(bf16[16,8448]{1,0:T(8,128)(2,1)} %copy.48), channel_id=1, source_target_pairs={{0,14},{2,0},{4,2},{6,4},{8,6},{10,8},{12,10},{14,12},{1,15},{3,1}... | collective-permute-start | bytes 811016 | tf_op jit(solution)/shard_map/ppermute | solution.py:57
  22.3 2.6 %all_gather.3 = bf16[16,8192]{1,0:T(8,128)(2,1)S(1)} all-gather(bf16[8,8192]{1,0:T(8,128)(2,1)S(1)} %copy-done.11), channel_id=1, replica_groups=mesh['dom'=16,'zz'=8,'cc'=2] {'cc'}, dimensions={0}, use_global_device_ids=true | all-gather | bytes 393216 | tf_op jit(solution)/shard_map/all_gather | solution.py:92
  24.9 5.8 %collective-permute-done.3 = bf16[16,8448]{1,0:T(8,128)(2,1)S(1)} collective-permute-done((bf16[16,8448]{1,0:T(8,128)(2,1)}, bf16[16,8448]{1,0:T(8,128)(2,1)S(1)}, u32[]{:S(2)}, u32[]{:S(2)}) %collective-permute-start.3) | collective-permute-done | bytes 270368 | tf_op jit(solution)/shard_map/ppermute | solution.py:54
  30.8 1.9 %multiply_add_fusion = (f32[25,16,4096]{2,1,0:T(8,128)S(1)}, f32[25,16,4096]{2,1,0:T(8,128)S(1)}) fusion(f32[16,4096]{1,0:T(8,128)S(1)} %get-tuple-element.31, f32[25,4096]{1,0:T(8,128)S(1)} %copy-done.1, f32[16,4096]{1,0:T(8,128)S(1)} %get-tuple-element.30, f32[25,4096]{1,0:T(8,128)S(1)} %copy-done.3), kind=kLoop, calls=%fused_computation.15 | loop fusion | flops 9830400 | bytes 14450688 | tf_op jit(solution)/shard_map/add | solution.py:130
  32.7 2.7 %collective-permute-start.1 = (bf16[16,8448]{1,0:T(8,128)(2,1)S(1)}, bf16[16,8448]{1,0:T(8,128)(2,1)}, u32[]{:S(2)}, u32[]{:S(2)}) collective-permute-start(bf16[16,8448]{1,0:T(8,128)(2,1)S(1)} %collective-permute-done), channel_id=1, source_target_pairs={{0,14},{2,0},{4,2},{6,4},{8,6},{10,8},{12,10},{14,12},{1,15},{3,1}... | collective-permute-start | bytes 811016 | tf_op jit(solution)/shard_map/ppermute | solution.py:57
  35.4 2.8 %collective-permute-done.4 = bf16[16,8448]{1,0:T(8,128)(2,1)S(1)} collective-permute-done((bf16[16,8448]{1,0:T(8,128)(2,1)S(1)}, bf16[16,8448]{1,0:T(8,128)(2,1)S(1)}, u32[]{:S(2)}, u32[]{:S(2)}) %collective-permute-start.4) | collective-permute-done | bytes 270368 | tf_op jit(solution)/shard_map/ppermute | solution.py:54
  38.2 5.7 %fusion.7 = (bf16[400,8192]{1,0:T(8,128)(2,1)}, bf16[400,8192]{1,0:T(8,128)(2,1)}) fusion(f32[400,4096]{1,0:T(8,128)S(1)} %bitcast.59, f32[400,4096]{1,0:T(8,128)S(1)} %bitcast.57), kind=kLoop, calls=%fused_computation.10 | loop fusion | flops 26214400 | bytes 26214400 | tf_op jit(solution)/shard_map/convert_element_type | solution.py:43
  43.9 2.7 %collective-permute-start.2 = (bf16[16,8448]{1,0:T(8,128)(2,1)}, bf16[16,8448]{1,0:T(8,128)(2,1)}, u32[]{:S(2)}, u32[]{:S(2)}) collective-permute-start(bf16[16,8448]{1,0:T(8,128)(2,1)} %collective-permute-done.1), channel_id=1, source_target_pairs={{0,14},{2,0},{4,2},{6,4},{8,6},{10,8},{12,10},{14,12},{1,15},{3,1}... | collective-permute-start | bytes 811016 | tf_op jit(solution)/shard_map/ppermute | solution.py:57
  46.7 3.3 %fusion.6 = bf16[400,8192]{1,0:T(8,128)(2,1)} fusion(f32[400,4096]{1,0:T(8,128)S(1)} %bitcast.60, f32[400,4096]{1,0:T(8,128)S(1)} %bitcast.58), kind=kLoop, calls=%fused_computation.9 | loop fusion | flops 13107200 | bytes 19660800 | tf_op jit(solution)/shard_map/convert_element_type | solution.py:41
  53.6 2.7 %copy.51 = bf16[16,8448]{0,1:T(8,128)(2,1)} copy(bf16[16,8448]{1,0:T(8,128)(2,1)} %collective-permute-done.1) | data formatting | bytes 540672 | tf_op jit(solution)/shard_map/ppermute | solution.py:57
  56.3 1.9 %copy.55 = bf16[16,8448]{0,1:T(8,128)(2,1)} copy(bf16[16,8448]{1,0:T(8,128)(2,1)S(1)} %copy-done.10) | data formatting | bytes 540672 | tf_op jit(solution)/shard_map/ppermute | solution.py:54
  58.2 2.7 %copy.54 = bf16[16,8448]{0,1:T(8,128)(2,1)} copy(bf16[16,8448]{1,0:T(8,128)(2,1)} %collective-permute-done.5) | data formatting | bytes 540672 | tf_op jit(solution)/shard_map/ppermute | solution.py:54
  60.9 2.7 %copy.52 = bf16[16,8448]{0,1:T(8,128)(2,1)} copy(bf16[16,8448]{1,0:T(8,128)(2,1)} %collective-permute-done.2) | data formatting | bytes 540672 | tf_op jit(solution)/shard_map/ppermute | solution.py:57
  63.5 2.7 %copy.53 = bf16[16,8448]{0,1:T(8,128)(2,1)} copy(bf16[16,8448]{1,0:T(8,128)(2,1)} %collective-permute-done.6) | data formatting | bytes 540672 | tf_op jit(solution)/shard_map/ppermute | solution.py:54
  66.2 16.4 %concatenate.38 = bf16[128,8448]{0,1:T(8,128)(2,1)} concatenate(bf16[16,8448]{0,1:T(8,128)(2,1)S(1)} %concatenate.37, bf16[16,8448]{0,1:T(8,128)(2,1)} %copy.50, bf16[16,8448]{0,1:T(8,128)(2,1)} %copy.51, bf16[16,8448]{0,1:T(8,128)(2,1)} %copy.52, bf16[16,8448]{0,1:T(8,128)(2,1)} %copy.53, bf16[16,8448]{0,1:T(8,128)(2,1)} %copy.54, bf16[16,8448]{0,1:T(8,128)(2,1)} %copy.55, ...), dimensions={0} | concatenate | bytes 4325376 | tf_op jit(solution)/shard_map/concatenate | solution.py:59
  83.3 10.3 %multiply_convert_fusion = (bf16[128,4096]{0,1:T(8,128)(2,1)S(1)}, bf16[128,4096]{0,1:T(8,128)(2,1)S(1)}, bf16[128,4096]{0,1:T(8,128)(2,1)S(1)}, bf16[128,4096]{...) fusion(f32[4096]{0:T(1024)S(1)} %copy-done.13, f32[128]{0:T(128)S(1)} %fusion.33, ...), kind=kLoop, calls=%fused_computation.32 | loop fusion | flops 9961472 | bytes 8438272 | tf_op jit(solution)/shard_map/convert_element_type | solution.py:113
  96.7 8.3 %fusion = f32[128,1200]{0,1:T(8,128)S(1)} fusion(bf16[128,8192]{0,1:T(8,128)(2,1)S(1)} %get-tuple-element.8, bf16[400,8192]{1,0:T(8,128)(2,1)S(1)} %bitcast.64, bf16[400,8192]{1,0:T(8,128)(2,1)S(1)} %bitcast.62, bf16[400,8192]{1,0:T(8,128)(2,1)} %fusion.6), kind=kOutput, calls=%fused_computation | convolution fusion | flops 2575564800 | bytes 22372352 | tf_op jit(solution)/shard_map/dot_general | solution.py:133
  105.9 3.9 %all-to-all-start = ((f32[8,2,128]{2,1,0:T(2,128)}), f32[8,2,128]{2,1,0:T(2,128)S(1)}, u32[]{:S(2)}, u32[]{:S(2)}) async-start(f32[8,2,128]{2,1,0:T(2,128)} %broadcast_in_dim.90), calls=%async_computation | async-start | bytes 16384 | tf_op jit(solution)/shard_map/all_to_all | solution.py:64
  109.9 6.6 %all-to-all-done = f32[8,2,128]{2,1,0:T(2,128)S(1)} async-done(((f32[8,2,128]{2,1,0:T(2,128)}), f32[8,2,128]{2,1,0:T(2,128)S(1)}, u32[]{:S(2)}, u32[]{:S(2)}) %all-to-all-start) | async-done | bytes 8224 | tf_op jit(solution)/shard_map/all_to_all | solution.py:64
  117.2 4.4 %fusion.8 = f32[25,16,12288]{2,1,0:T(8,128)S(1)} fusion(bf16[25,16,128]{2,1,0:T(8,128)(2,1)S(1)} %bitcast.68, bf16[128,4096]{0,1:T(8,128)(2,1)S(1)} %get-tuple-element.11, bf16[128,8192]{0,1:T(8,128)(2,1)} %get-tuple-element.10), kind=kOutput, calls=%fused_computation.17 | convolution fusion | flops 1264582656 | bytes 22908928 | tf_op jit(solution)/shard_map/dot_general | solution.py:160
  121.6 2.8 %subtract_reduce_fusion = (f32[16,4096]{1,0:T(8,128)S(1)}, f32[16,4096]{1,0:T(8,128)S(1)}, f32[16,4096]{1,0:T(8,128)S(1)}) fusion(f32[25,16,12288]{2,1,0:T(8,128)S(1)} %fusion.8, f32[25,4096]{1,0:T(8,128)S(1)} %copy-done.2, f32[25,4096]{1,0:T(8,128)S(1)} %copy-done.4), kind=kLoop, calls=%fused_computation.13 | loop fusion | flops 14548992 | bytes 21266432 | tf_op jit(solution)/shard_map/reduce_sum | solution.py:169
  124.5 25.6 %all_to_all.10 = f32[32,8,768]{2,1,0:T(8,128)S(1)} all-to-all(f32[32,8,768]{2,1,0:T(8,128)S(1)} %bitcast.65), channel_id=1, replica_groups=mesh['dom'=16,'zz'=8,'cc'=2] {'cc','dom'}, dimensions={0} | all-to-all | bytes 1572864 | tf_op jit(solution)/shard_map/all_to_all | solution.py:185
  (83 shorter events, 14.6 us)
Async XLA Ops:
  0.6 30.2 %copy-start.1 = (f32[25,4096]{1,0:T(8,128)S(1)}, f32[25,4096]{1,0:T(8,128)}, u32[]{:S(2)}) copy-start(f32[25,4096]{1,0:T(8,128)} %constant.78.clone) | copy-start | bytes 1228804
  0.6 30.2 %copy-start.3 = (f32[25,4096]{1,0:T(8,128)S(1)}, f32[25,4096]{1,0:T(8,128)}, u32[]{:S(2)}) copy-start(f32[25,4096]{1,0:T(8,128)} %constant.77.clone) | copy-start | bytes 1228804
  0.7 21.6 %copy-start.11 = (bf16[8,8192]{1,0:T(8,128)(2,1)S(1)}, bf16[8,8192]{1,0:T(8,128)(2,1)}, u32[]{:S(2)}) copy-start(bf16[8,8192]{1,0:T(8,128)(2,1)} %param.14) | copy-start | bytes 393220
  15.9 16.8 %collective-permute-start = (bf16[16,8448]{1,0:T(8,128)(2,1)}, bf16[16,8448]{1,0:T(8,128)(2,1)S(1)}, u32[]{:S(2)}, u32[]{:S(2)}) collective-permute-start(bf16[16,8448]{1,0:T(8,128)(2,1)} %copy.48), channel_id=1, source_target_pairs={{0,14},{2,0},{4,2},{6,4},{8,6},{10,8},{12,10},{14,12},{1,15},{3,1}... | collective-permute-start | bytes 811016 | tf_op jit(solution)/shard_map/ppermute | solution.py:57
  22.3 8.5 %collective-permute-start.3 = (bf16[16,8448]{1,0:T(8,128)(2,1)}, bf16[16,8448]{1,0:T(8,128)(2,1)S(1)}, u32[]{:S(2)}, u32[]{:S(2)}) collective-permute-start(bf16[16,8448]{1,0:T(8,128)(2,1)} %copy.48), channel_id=1, source_target_pairs={{0,2},{2,4},{4,6},{6,8},{8,10},{10,12},{12,14},{14,0},{1,3},{3,5},... | collective-permute-start | bytes 811016 | tf_op jit(solution)/shard_map/ppermute | solution.py:54
  30.8 7.4 %collective-permute-start.4 = (bf16[16,8448]{1,0:T(8,128)(2,1)S(1)}, bf16[16,8448]{1,0:T(8,128)(2,1)S(1)}, u32[]{:S(2)}, u32[]{:S(2)}) collective-permute-start(bf16[16,8448]{1,0:T(8,128)(2,1)S(1)} %collective-permute-done.3), channel_id=1, source_target_pairs={{0,2},{2,4},{4,6},{6,8},{8,10},{10,12},{12,14},{14,0},{1,3},{3,5},... | collective-permute-start | bytes 811016 | tf_op jit(solution)/shard_map/ppermute | solution.py:54
  32.7 11.2 %copy-start.5 = (bf16[16,8448]{1,0:T(8,128)(2,1)}, bf16[16,8448]{1,0:T(8,128)(2,1)S(1)}, u32[]{:S(2)}) copy-start(bf16[16,8448]{1,0:T(8,128)(2,1)S(1)} %collective-permute-done) | copy-start | bytes 811012
  32.7 11.2 %collective-permute-start.1 = (bf16[16,8448]{1,0:T(8,128)(2,1)S(1)}, bf16[16,8448]{1,0:T(8,128)(2,1)}, u32[]{:S(2)}, u32[]{:S(2)}) collective-permute-start(bf16[16,8448]{1,0:T(8,128)(2,1)S(1)} %collective-permute-done), channel_id=1, source_target_pairs={{0,14},{2,0},{4,2},{6,4},{8,6},{10,8},{12,10},{14,12},{1,15},{3,1}... | collective-permute-start | bytes 811016 | tf_op jit(solution)/shard_map/ppermute | solution.py:57
  38.2 5.7 %copy-start.9 = (bf16[16,8448]{1,0:T(8,128)(2,1)}, bf16[16,8448]{1,0:T(8,128)(2,1)S(1)}, u32[]{:S(2)}) copy-start(bf16[16,8448]{1,0:T(8,128)(2,1)S(1)} %collective-permute-done.4) | copy-start | bytes 811012
  38.2 8.4 %collective-permute-start.5 = (bf16[16,8448]{1,0:T(8,128)(2,1)S(1)}, bf16[16,8448]{1,0:T(8,128)(2,1)}, u32[]{:S(2)}, u32[]{:S(2)}) collective-permute-start(bf16[16,8448]{1,0:T(8,128)(2,1)S(1)} %collective-permute-done.4), channel_id=1, source_target_pairs={{0,2},{2,4},{4,6},{6,8},{8,10},{10,12},{12,14},{14,0},{1,3},{3,5},... | collective-permute-start | bytes 811016 | tf_op jit(solution)/shard_map/ppermute | solution.py:54
  43.9 6.0 %copy-start.12 = (f32[4096]{0:T(1024)S(1)}, f32[4096]{0:T(1024)}, u32[]{:S(2)}) copy-start(f32[4096]{0:T(1024)} %param.13) | copy-start | bytes 49156
  43.9 7.9 %copy-start.8 = (bf16[16,8448]{1,0:T(8,128)(2,1)S(1)}, bf16[16,8448]{1,0:T(8,128)(2,1)}, u32[]{:S(2)}) copy-start(bf16[16,8448]{1,0:T(8,128)(2,1)} %copy-done.7) | copy-start | bytes 811012
  43.9 6.0 %copy-start.6 = (bf16[16,8448]{1,0:T(8,128)(2,1)S(1)}, bf16[16,8448]{1,0:T(8,128)(2,1)}, u32[]{:S(2)}) copy-start(bf16[16,8448]{1,0:T(8,128)(2,1)} %copy-done.5) | copy-start | bytes 811012
  43.9 16.9 %collective-permute-start.2 = (bf16[16,8448]{1,0:T(8,128)(2,1)}, bf16[16,8448]{1,0:T(8,128)(2,1)}, u32[]{:S(2)}, u32[]{:S(2)}) collective-permute-start(bf16[16,8448]{1,0:T(8,128)(2,1)} %collective-permute-done.1), channel_id=1, source_target_pairs={{0,14},{2,0},{4,2},{6,4},{8,6},{10,8},{12,10},{14,12},{1,15},{3,1}... | collective-permute-start | bytes 811016 | tf_op jit(solution)/shard_map/ppermute | solution.py:57
  46.7 16.9 %collective-permute-start.6 = (bf16[16,8448]{1,0:T(8,128)(2,1)}, bf16[16,8448]{1,0:T(8,128)(2,1)}, u32[]{:S(2)}, u32[]{:S(2)}) collective-permute-start(bf16[16,8448]{1,0:T(8,128)(2,1)} %collective-permute-done.5), channel_id=1, source_target_pairs={{0,2},{2,4},{4,6},{6,8},{8,10},{10,12},{12,14},{14,0},{1,3},{3,5},... | collective-permute-start | bytes 811016 | tf_op jit(solution)/shard_map/ppermute | solution.py:54
  49.9 6.4 %copy-start.10 = (bf16[16,8448]{1,0:T(8,128)(2,1)S(1)}, bf16[16,8448]{1,0:T(8,128)(2,1)}, u32[]{:S(2)}) copy-start(bf16[16,8448]{1,0:T(8,128)(2,1)} %copy-done.9) | copy-start | bytes 811012
  66.2 17.1 %copy-start.13 = (f32[4096]{0:T(1024)S(1)}, f32[4096]{0:T(1024)}, u32[]{:S(2)}) copy-start(f32[4096]{0:T(1024)} %constant.79.clone) | copy-start | bytes 49156
  83.2 12.5 %slice-start.1 = ((s8[6553600]{0:T(1024)(128)(4,1)}), s8[4194304]{0:T(1024)(128)(4,1)S(1)}, s32[]{:S(2)}) async-start(s8[6553600]{0:T(1024)(128)(4,1)} %bitcast.61), calls=%async_computation.3 | async-start | bytes 8388608
  83.3 12.5 %slice-start.3 = ((s8[6553600]{0:T(1024)(128)(4,1)}), s8[4194304]{0:T(1024)(128)(4,1)S(1)}, s32[]{:S(2)}) async-start(s8[6553600]{0:T(1024)(128)(4,1)} %bitcast.63), calls=%async_computation.5 | async-start | bytes 8388608
  93.6 3.1 %slice-start.4 = ((s8[6553600]{0:T(1024)(128)(4,1)}), s8[2359296]{0:T(1024)(128)(4,1)S(1)}, s32[]{:S(2)}) async-start(s8[6553600]{0:T(1024)(128)(4,1)} %bitcast.63), calls=%async_computation.6 | async-start | bytes 4718592
  96.7 13.1 %copy-start = (bf16[128,8448]{0,1:T(8,128)(2,1)S(1)}, bf16[128,8448]{0,1:T(8,128)(2,1)}, u32[]{:S(2)}) copy-start(bf16[128,8448]{0,1:T(8,128)(2,1)} %concatenate.38) | copy-start | bytes 6488068
  105.9 10.5 %all-to-all-start = ((f32[8,2,128]{2,1,0:T(2,128)}), f32[8,2,128]{2,1,0:T(2,128)S(1)}, u32[]{:S(2)}, u32[]{:S(2)}) async-start(f32[8,2,128]{2,1,0:T(2,128)} %broadcast_in_dim.90), calls=%async_computation | async-start | bytes 16384 | tf_op jit(solution)/shard_map/all_to_all | solution.py:64
  117.2 4.4 %copy-start.2 = (f32[25,4096]{1,0:T(8,128)S(1)}, f32[25,4096]{1,0:T(8,128)}, u32[]{:S(2)}) copy-start(f32[25,4096]{1,0:T(8,128)} %constant.78.clone) | copy-start | bytes 1228804
  117.2 4.4 %copy-start.4 = (f32[25,4096]{1,0:T(8,128)S(1)}, f32[25,4096]{1,0:T(8,128)}, u32[]{:S(2)}) copy-start(f32[25,4096]{1,0:T(8,128)} %constant.77.clone) | copy-start | bytes 1228804
  (3 other events, 6.5 us)

commit v3 on v1

--- a/solution.py
+++ b/solution.py
@@ -45,6 +45,11 @@
     return first, second, third
 
 
+def exchange(values, axis, size):
+    spread = jnp.broadcast_to(values[None], (size,) + values.shape)
+    return lax.all_to_all(spread, axis, 0, 0, tiled=True)
+
+
 def shards(images, defocus, inv_noise, slices, lists, counts):
     rows = images.shape[0]
     own_orients = slices.shape[0]
@@ -52,7 +57,6 @@
     pad = (-(orient_total + 2)) % 128
     zz = lax.axis_index("zz")
     cc = lax.axis_index("cc")
-    group = lax.axis_size("zz")
 
     orient_ids = jnp.arange(orient_total, dtype=jnp.int32)
     slot_live = jnp.arange(lists.shape[1], dtype=jnp.int32)[None, :] < counts[:, None]
@@ -68,30 +72,34 @@
         ),
         axis=1,
     )
-    packed = jnp.concatenate((images, extra), axis=1)
-    gathered = lax.all_gather(packed, "zz", axis=0, tiled=True)
+    first = jnp.concatenate((images[:, :COEF], extra), axis=1)
+    group = lax.axis_size("zz")
+    gathered = lax.all_gather(first, "zz", axis=0, tiled=True)
+    g_imag = lax.all_gather(images[:, COEF:], "zz", axis=0, tiled=True)
     local_slices = lax.all_gather(slices, "cc", axis=0, tiled=True)
     count = gathered.shape[0]
     chip_orients = local_slices.shape[0]
 
-    g_images = gathered[:, :PIX]
-    g_mask_all = gathered[:, PIX : PIX + orient_total]
-    g_alive = gathered[:, PIX + orient_total] > 0.5
-    g_defocus = gathered[:, PIX + orient_total + 1].astype(jnp.float32)
+    g_mask_all = gathered[:, COEF : COEF + orient_total]
+    g_alive = gathered[:, COEF + orient_total] > 0.5
+    g_defocus = gathered[:, COEF + orient_total + 1].astype(jnp.float32)
     mask = lax.dynamic_slice_in_dim(g_mask_all, zz * chip_orients, chip_orients, 1) > 0.5
 
     cosine = jnp.asarray(COSINE)
     sine = jnp.asarray(SINE)
     radius = jnp.asarray(RADIUS)
     ctf = -jnp.sin(jnp.pi * g_defocus[:, None] * radius[None, :] + 0.1)
-    real_part = g_images[:, :COEF].astype(jnp.float32)
-    imag_part = g_images[:, COEF:].astype(jnp.float32)
-    weighted = jnp.concatenate(
-        (inv_noise * ctf * real_part, inv_noise * ctf * imag_part), axis=-1
-    ).astype(jnp.bfloat16)
-    image_half = jnp.concatenate((ctf * real_part, ctf * imag_part), axis=-1).astype(jnp.bfloat16)
     quad_half = (-0.5 * inv_noise * ctf * ctf).astype(jnp.bfloat16)
     ctf_half = (ctf * ctf).astype(jnp.bfloat16)
+    real_part = gathered[:, :COEF].astype(jnp.float32)
+    weighted_r = (inv_noise * ctf * real_part).astype(jnp.bfloat16)
+    image_r = (ctf * real_part).astype(jnp.bfloat16)
+    ctf, weighted_r, image_r, quad_half, ctf_half = lax.optimization_barrier(
+        (ctf, weighted_r, image_r, quad_half, ctf_half)
+    )
+    imag_part = g_imag.astype(jnp.float32)
+    weighted_i = (inv_noise * ctf * imag_part).astype(jnp.bfloat16)
+    image_i = (ctf * imag_part).astype(jnp.bfloat16)
 
     slices_wide = local_slices.astype(jnp.float32)
     squares = (slices_wide * slices_wide).astype(jnp.bfloat16)
@@ -105,13 +113,16 @@
     s_imag = slices_wide[None, :, COEF:]
     c_t = cosine[:, None, :]
     s_t = sine[:, None, :]
-    turned = jnp.concatenate((c_t * s_real + s_t * s_imag, c_t * s_imag - s_t * s_real), axis=-1)
-    turned = turned.reshape(TRANS * chip_orients, PIX)
-    parts = jnp.concatenate(split3(turned), axis=0)
+    block = TRANS * chip_orients
+    turned_r = (c_t * s_real + s_t * s_imag).reshape(block, COEF)
+    turned_i = (c_t * s_imag - s_t * s_real).reshape(block, COEF)
+    parts_r = jnp.concatenate(split3(turned_r), axis=0)
+    parts_i = jnp.concatenate(split3(turned_i), axis=0)
     linear3 = lax.dot_general(
-        weighted, parts, (((1,), (1,)), ((), ())), preferred_element_type=jnp.float32
+        weighted_r, parts_r, (((1,), (1,)), ((), ())), preferred_element_type=jnp.float32
+    ) + lax.dot_general(
+        weighted_i, parts_i, (((1,), (1,)), ((), ())), preferred_element_type=jnp.float32
     )
-    block = TRANS * chip_orients
     linear = linear3[:, :block] + linear3[:, block : 2 * block] + linear3[:, 2 * block :]
     linear = linear.reshape(count, TRANS, chip_orients)
     score = jnp.where(mask[:, None, :], linear + energy[:, None, :], SENTINEL)
@@ -120,7 +131,7 @@
     local_sum = jnp.sum(
         jnp.where(mask[:, None, :], jnp.exp(score - local_max[:, None, None]), 0.0), axis=(1, 2)
     )
-    stats = lax.all_gather(jnp.stack((local_max, local_sum)), "zz", axis=0)
+    stats = exchange(jnp.stack((local_max, local_sum)), "zz", group)
     highest = jnp.max(stats[:, 0], axis=0)
     normalizer = jnp.sum(stats[:, 1] * jnp.exp(stats[:, 0] - highest[None, :]), axis=0)
     highest = jnp.where(g_alive, highest, 0.0)
@@ -133,18 +144,18 @@
 
     flat_post = posterior.reshape(count, block)
     accum = lax.dot_general(
-        flat_post, image_half, (((0,), (0,)), ((), ())), preferred_element_type=jnp.float32
-    ).reshape(TRANS, chip_orients, PIX)
+        flat_post,
+        jnp.concatenate((image_r, image_i, ctf_half), axis=1),
+        (((0,), (0,)), ((), ())),
+        preferred_element_type=jnp.float32,
+    ).reshape(TRANS, chip_orients, PIX + COEF)
+    weight = jnp.sum(accum[:, :, PIX:], axis=0)
     a_real = accum[:, :, :COEF]
-    a_imag = accum[:, :, COEF:]
+    a_imag = accum[:, :, COEF:PIX]
     data_real = jnp.sum(c_t * a_real - s_t * a_imag, axis=0)
     data_imag = jnp.sum(s_t * a_real + c_t * a_imag, axis=0)
     data = jnp.concatenate((data_real, data_imag), axis=-1)
 
-    per_orient = jnp.sum(posterior.astype(jnp.float32), axis=1)
-    weight = lax.dot_general(
-        per_orient, ctf_half.astype(jnp.float32), (((0,), (0,)), ((), ())), precision=HIGHEST
-    )
 
     doms = lax.axis_size("dom")
     halves = lax.axis_size("cc")
@@ -155,7 +166,9 @@
     both = jnp.concatenate((data_b, weight_b), axis=-1).reshape(
         halves * doms * own_orients, data_cols + weight_cols
     )
-    reduced = lax.psum_scatter(both, ("cc", "dom"), scatter_dimension=0, tiled=True)
+    pieces = halves * doms
+    both = both.reshape(pieces, own_orients, data_cols + weight_cols)
+    reduced = jnp.sum(lax.all_to_all(both, ("cc", "dom"), 0, 0, tiled=True), axis=0)
     data_out = reduced[:, :data_cols]
     weight_out = reduced[:, data_cols:]
     return (peak_weight, data_out, weight_out)

time: 216 us -> 151 us (0.70)
  waiting for transfers between devices: 113 us -> 47.2 us
  starting transfers between devices: 0.08 us -> 17.9 us
  matrix products: 36 us -> 20.7 us
  blocking collectives: 16.6 us -> 5.04 us
  other arithmetic: 29.3 us -> 38.9 us
    reduce_scatter x1 -> x0, waiting for transfers between devices: 90 us -> none  [shards(): lax.psum_scatter(both, ('cc', 'dom'), scatter_dimension=0, tiled=True)]
    all_to_all x0 -> x2, starting transfers between devices: none -> 17.8 us  [the longest x1 13.4 us: shards(): lax.all_to_all(both, ('cc', 'dom'), 0, 0, tiled=True)]
    all_to_all x0 -> x2, waiting for transfers between devices: none -> 17.4 us  [the longest x1 13.2 us: shards(): lax.all_to_all(both, ('cc', 'dom'), 0, 0, tiled=True)]
    convert_element_type x0 -> x2, other arithmetic: none -> 12 us  [the longest x1 10.6 us: shards(): ctf_half = (ctf * ctf).astype(jnp.bfloat16)]
    all_gather x1 -> x0, blocking collectives: 11.6 us -> none  [shards(): stats = lax.all_gather(jnp.stack((local_max, local_sum)), 'zz', axis=0)]
    another operation x1, other arithmetic: 9.27 us -> 0.01 us  [shards(): stats = exchange(jnp.stack((local_max, local_sum)), 'zz', group)]
    dot_general x1, matrix products: 7.62 us -> 1.29 us  [shards(): lax.dot_general(quad_half, squares[:, COEF:], (((1,), (1,)), ((), ())), p...]
    dot_general x1, matrix products: 7.43 us -> 1.3 us  [shards(): lax.dot_general(quad_half, squares[:, :COEF], (((1,), (1,)), ((), ())), p...]
  transfers between devices with their start and end apart: 2 -> 4, of which waited for: 2 -> 4; matrix products, arithmetic and copies ran while one was open for 6% -> 29% of each run, Pallas kernels for 0% -> 0%
where the time goes in v3:
time: 151 us; the launch traced here: 150 us
  waiting for transfers between devices  47.2 us (31%)
  other arithmetic  38.9 us (26%)
  matrix products  20.7 us (14%)
  starting transfers between devices  17.9 us (12%)
  between operations  14.2 us (9%)
  local copies, waits for them, and re-layouts  6.36 us (4%)
  blocking collectives  5.04 us (3%)
    all_gather x1, waiting for transfers between devices, shards(): g_imag = lax.all_gather(images[:, COEF:], 'zz', axis=0, tiled=True)  16.4 us
    all_to_all x1, starting transfers between devices, shards(): lax.all_to_all(both, ('cc', 'dom'), 0, 0, tiled=True)  13.4 us
    all_to_all x1, waiting for transfers between devices, shards(): lax.all_to_all(both, ('cc', 'dom'), 0, 0, tiled=True)  13.2 us
    all_gather x1, waiting for transfers between devices, shards(): gathered = lax.all_gather(first, 'zz', axis=0, tiled=True)  12.6 us
    convert_element_type x1, other arithmetic, shards(): ctf_half = (ctf * ctf).astype(jnp.bfloat16)  10.6 us
    convert_element_type x2, other arithmetic, split3(): second = rest.astype(jnp.bfloat16)  7.96 us
    dot_general x1, matrix products, shards(): lax.dot_general(weighted_r, parts_r, (((1,), (1,)), ((), ())), preferred_...  7.86 us
    convert_element_type x1, other arithmetic, split3(): first = values.astype(jnp.bfloat16)  7.04 us
  transfers between devices with their start and end apart: 4, of which 4 were waited for; matrix products, arithmetic and copies ran while one was open for 29% of the time, Pallas kernels for 0%

profile of v3, /device:TPU:1, one launch (start us, length us, event | category | flops | bytes accessed | tf_op | source)
XLA Modules:
  0.0 150.2 jit_solution(8029037291587683371)
XLA Ops:
  8.6 1.6 %fusion.45 = (bf16[16,4096]{1,0:T(8,128)(2,1)}, bf16[16,4096]{1,0:T(8,128)(2,1)S(1)}) fusion(bf16[16,8192]{1,0:T(8,128)(2,1)} %param.9), kind=kLoop, calls=%fused_computation.83 | loop fusion | bytes 524288 | tf_op jit(solution)/shard_map/slice | solution.py:78
  10.2 0.9 fusion.31
  13.5 5.0 %all_gather.10 = bf16[16,8192]{1,0:T(8,128)(2,1)S(1)} all-gather(bf16[8,8192]{1,0:T(8,128)(2,1)} %param.12), channel_id=1, replica_groups=mesh['dom'=16,'zz'=8,'cc'=2] {'cc'}, dimensions={0}, use_global_device_ids=true | all-gather | bytes 393216 | tf_op jit(solution)/shard_map/all_gather | solution.py:79
  19.4 2.9 %multiply_subtract_fusion = (f32[25,16,4096]{2,1,0:T(8,128)S(1)}, f32[25,16,4096]{2,1,0:T(8,128)S(1)}) fusion(f32[16,4096]{1,0:T(8,128)S(1)} %get-tuple-element.29, f32[25,4096]{1,0:T(8,128)} %constant.17.clone, f32[16,4096]{1,0:T(8,128)S(1)} %get-tuple-element.28, f32[25,4096]{1,0:T(8,128)} %constant.16.clone), kind=kLoop, calls=%fused_computation.20 | loop fusion | flops 9830400 | bytes 14450688 | tf_op jit(solution)/shard_map/sub | solution.py:118
  22.3 4.1 %fusion.12 = (bf16[400,4096]{1,0:T(8,128)(2,1)}, bf16[400,4096]{1,0:T(8,128)(2,1)}) fusion(f32[25,16,4096]{2,1,0:T(8,128)S(1)} %get-tuple-element.23), kind=kLoop, calls=%fused_computation.23 | loop fusion | flops 11468800 | bytes 13107200 | tf_op jit(solution)/shard_map/convert_element_type | solution.py:43
  27.0 7.0 %bitcast_convert_fusion = (bf16[400,4096]{1,0:T(8,128)(2,1)}, bf16[400,4096]{1,0:T(8,128)(2,1)}) fusion(f32[25,16,4096]{2,1,0:T(8,128)S(1)} %get-tuple-element.22, f32[25,16,4096]{2,1,0:T(8,128)} %copy-done), kind=kLoop, calls=%fused_computation.14 | loop fusion | flops 3276800 | bytes 19660800 | tf_op jit(solution)/shard_map/convert_element_type | solution.py:41
  34.0 3.8 %fusion.13 = (bf16[400,4096]{1,0:T(8,128)(2,1)}, bf16[400,4096]{1,0:T(8,128)(2,1)}) fusion(f32[25,16,4096]{2,1,0:T(8,128)S(1)} %get-tuple-element.22), kind=kLoop, calls=%fused_computation.24 | loop fusion | flops 11468800 | bytes 13107200 | tf_op jit(solution)/shard_map/convert_element_type | solution.py:43
  37.9 12.6 %all-gather.3.cloned.1.call-done = bf16[128,4352]{1,0:T(8,128)(2,1)} async-done(((bf16[16,4352]{1,0:T(8,128)(2,1)}), bf16[128,4352]{1,0:T(8,128)(2,1)}) %all-gather.3.cloned.1.call-update) | async-done | bytes 1114128 | tf_op jit(solution)/shard_map/all_gather | solution.py:77
  50.5 0.9 multiply_reduce_fusion
  51.4 10.6 %multiply_convert_fusion = (bf16[128,4096]{1,0:T(8,128)(2,1)}, bf16[128,4096]{1,0:T(8,128)(2,1)S(1)}, bf16[128,4096]{1,0:T(8,128)(2,1)}, bf16[128,4096]{1,0:T(8,128)(2,1)}, f32[128,4096]{1,0:T(8,128)S(1)}) fusion(f32[4096]{0:T(1024)S(1)} %copy-done.4, f32[128]{0:T(128)S(1)} %multiply_reduce_fusion, f32[4096]{0:T(1024)S(1)} %broadcast_multiply_fusion, ...), kind=kLoop, calls=%fused_computation.42 | loop fusion | flops 7340032 | bytes 7389696 | tf_op jit(solution)/shard_map/convert_element_type | solution.py:93
  62.2 1.3 fusion.37
  63.5 1.3 convolution_add_fusion
  64.8 7.9 %fusion = f32[128,1200]{0,1:T(8,128)} fusion(bf16[128,4096]{1,0:T(8,128)(2,1)} %get-tuple-element.8, bf16[400,4096]{1,0:T(8,128)(2,1)} %get-tuple-element.21, bf16[400,4096]{1,0:T(8,128)(2,1)} %get-tuple-element.20, bf16[400,4096]{1,0:T(8,128)(2,1)} %get-tuple-element.41), kind=kOutput, calls=%fused_computation | convolution fusion | flops 1287782400 | bytes 11493376 | tf_op jit(solution)/shard_map/dot_general | solution.py:121
  72.6 16.4 %all-gather.5.cloned.1.call-done = bf16[128,4096]{1,0:T(8,128)(2,1)} async-done(((bf16[16,4096]{1,0:T(8,128)(2,1)}), bf16[128,4096]{1,0:T(8,128)(2,1)}) %all-gather.5.cloned.1.call-update) | async-done | bytes 1048592 | tf_op jit(solution)/shard_map/all_gather | solution.py:78
  89.0 5.9 %fusion.19 = f32[128,1200]{0,1:T(8,128)S(1)} fusion(f32[128,1200]{0,1:T(8,128)} %fusion, bf16[400,4096]{1,0:T(8,128)(2,1)} %get-tuple-element.19, bf16[400,4096]{1,0:T(8,128)(2,1)} %get-tuple-element.18, bf16[400,4096]{1,0:T(8,128)(2,1)} %get-tuple-element.40, bf16[128,4096]{1,0:T(8,128)(2,1)} %all-gather.5.cloned.1.call-done, ...), kind=kOutput, calls=%fused_computation.36 | convolution fusion | flops 1290033152 | bytes 14221312 | tf_op jit(solution)/shard_map/dot_general | solution.py:123
  95.7 4.5 %all-to-all-start = ((f32[8,2,128]{2,1,0:T(2,128)}), f32[8,2,128]{2,1,0:T(2,128)S(1)}, u32[]{:S(2)}, u32[]{:S(2)}) async-start(f32[8,2,128]{2,1,0:T(2,128)} %broadcast_in_dim.90), calls=%async_computation | async-start | bytes 16384 | tf_op jit(solution)/shard_map/all_to_all | solution.py:50
  100.1 1.4 fusion.25
  101.6 0.9 compare_reduce_fusion
  102.4 4.3 %all-to-all-done = f32[8,2,128]{2,1,0:T(2,128)S(1)} async-done(((f32[8,2,128]{2,1,0:T(2,128)}), f32[8,2,128]{2,1,0:T(2,128)S(1)}, u32[]{:S(2)}, u32[]{:S(2)}) %all-to-all-start) | async-done | bytes 8224 | tf_op jit(solution)/shard_map/all_to_all | solution.py:50
  106.9 4.3 %fusion.14 = f32[25,16,12288]{2,1,0:T(8,128)S(1)} fusion(bf16[25,16,128]{2,1,0:T(8,128)(2,1)S(1)} %bitcast.71, bf16[128,4096]{1,0:T(8,128)(2,1)} %get-tuple-element.12, bf16[128,4096]{1,0:T(8,128)(2,1)S(1)} %fusion.25, bf16[128,4096]{1,0:T(8,128)(2,1)} %get-tuple-element.11), kind=kOutput, calls=%fused_computation.26 | convolution fusion | flops 1267728384 | bytes 22908928 | tf_op jit(solution)/shard_map/dot_general | solution.py:146
  111.2 2.8 %subtract_reduce_fusion = (f32[16,4096]{1,0:T(8,128)S(1)}, f32[16,4096]{1,0:T(8,128)S(1)}, f32[16,4096]{1,0:T(8,128)S(1)}) fusion(f32[25,16,12288]{2,1,0:T(8,128)S(1)} %fusion.14, f32[25,4096]{1,0:T(8,128)S(1)} %copy-done.1, f32[25,4096]{1,0:T(8,128)S(1)} %copy-done.2), kind=kLoop, calls=%fused_computation.18 | loop fusion | flops 14548992 | bytes 21266432 | tf_op jit(solution)/shard_map/reduce_sum | solution.py:155
  114.1 0.9 pad_maximum_fusion
  115.0 13.4 %all-to-all-start.1 = ((f32[32,8,768]{2,1,0:T(8,128)}), f32[32,8,768]{2,1,0:T(8,128)S(1)}, u32[]{:S(2)}, u32[]{:S(2)}) async-start(f32[32,8,768]{2,1,0:T(8,128)} %bitcast.18), calls=%async_computation.1 | async-start | bytes 1572864 | tf_op jit(solution)/shard_map/all_to_all | solution.py:171
  129.0 13.2 %all-to-all-done.1 = f32[32,8,768]{2,1,0:T(8,128)S(1)} async-done(((f32[32,8,768]{2,1,0:T(8,128)}), f32[32,8,768]{2,1,0:T(8,128)S(1)}, u32[]{:S(2)}, u32[]{:S(2)}) %all-to-all-start.1) | async-done | bytes 786464 | tf_op jit(solution)/shard_map/all_to_all | solution.py:171
  (43 shorter events, 8.1 us)
Async XLA Ops:
  7.2 43.3 %all-gather.3.cloned.1.call-start = ((), (), s32[]{:S(2)}) async-start(), calls=%async_computation.2 | async-start | bytes 1253376 | tf_op jit(solution)/shard_map/all_gather | solution.py:77
  12.8 76.2 %all-gather.5.cloned.1.call-start = ((), (), s32[]{:S(2)}) async-start(), calls=%async_computation.3 | async-start | bytes 1179648 | tf_op jit(solution)/shard_map/all_gather | solution.py:78
  22.3 4.7 %copy-start = (f32[25,16,4096]{2,1,0:T(8,128)}, f32[25,16,4096]{2,1,0:T(8,128)S(1)}, u32[]{:S(2)}) copy-start(f32[25,16,4096]{2,1,0:T(8,128)S(1)} %get-tuple-element.23) | copy-start | bytes 19660804
  34.0 3.8 %copy-start.3 = (f32[4096]{0:T(1024)S(1)}, f32[4096]{0:T(1024)}, u32[]{:S(2)}) copy-start(f32[4096]{0:T(1024)} %param.11) | copy-start | bytes 49156
  34.0 17.4 %copy-start.4 = (f32[4096]{0:T(1024)S(1)}, f32[4096]{0:T(1024)}, u32[]{:S(2)}) copy-start(f32[4096]{0:T(1024)} %constant.44.clone) | copy-start | bytes 49156
  50.5 11.5 %slice-start = ((bf16[128,4352]{1,0:T(8,128)(2,1)}), bf16[128,128]{1,0:T(8,128)(2,1)S(1)}, s32[]{:S(2)}) async-start(bf16[128,4352]{1,0:T(8,128)(2,1)} %all-gather.3.cloned.1.call-done), calls=%async_computation.4 | async-start | bytes 65536 | tf_op jit(solution)/shard_map/slice | solution.py:83
  95.7 11.0 %all-to-all-start = ((f32[8,2,128]{2,1,0:T(2,128)}), f32[8,2,128]{2,1,0:T(2,128)S(1)}, u32[]{:S(2)}, u32[]{:S(2)}) async-start(f32[8,2,128]{2,1,0:T(2,128)} %broadcast_in_dim.90), calls=%async_computation | async-start | bytes 16384 | tf_op jit(solution)/shard_map/all_to_all | solution.py:50
  106.8 4.4 %copy-start.1 = (f32[25,4096]{1,0:T(8,128)S(1)}, f32[25,4096]{1,0:T(8,128)}, u32[]{:S(2)}) copy-start(f32[25,4096]{1,0:T(8,128)} %constant.17.clone) | copy-start | bytes 1228804
  106.9 4.4 %copy-start.2 = (f32[25,4096]{1,0:T(8,128)S(1)}, f32[25,4096]{1,0:T(8,128)}, u32[]{:S(2)}) copy-start(f32[25,4096]{1,0:T(8,128)} %constant.16.clone) | copy-start | bytes 1228804
  115.0 27.1 %all-to-all-start.1 = ((f32[32,8,768]{2,1,0:T(8,128)}), f32[32,8,768]{2,1,0:T(8,128)S(1)}, u32[]{:S(2)}, u32[]{:S(2)}) async-start(f32[32,8,768]{2,1,0:T(8,128)} %bitcast.18), calls=%async_computation.1 | async-start | bytes 1572864 | tf_op jit(solution)/shard_map/all_to_all | solution.py:171
Sparse Core Ops, SparseCore 0:
  12.9 37.5 all-gather.2
  52.3 36.7 all-gather.4

commit v4 on v3

--- a/solution.py
+++ b/solution.py
@@ -72,17 +72,16 @@
         ),
         axis=1,
     )
-    first = jnp.concatenate((images[:, :COEF], extra), axis=1)
     group = lax.axis_size("zz")
-    gathered = lax.all_gather(first, "zz", axis=0, tiled=True)
-    g_imag = lax.all_gather(images[:, COEF:], "zz", axis=0, tiled=True)
+    meta = exchange(extra, "zz", group).reshape(group * rows, extra.shape[1])
+    g_images = lax.all_gather(images, "zz", axis=0, tiled=True)
     local_slices = lax.all_gather(slices, "cc", axis=0, tiled=True)
-    count = gathered.shape[0]
+    count = g_images.shape[0]
     chip_orients = local_slices.shape[0]
 
-    g_mask_all = gathered[:, COEF : COEF + orient_total]
-    g_alive = gathered[:, COEF + orient_total] > 0.5
-    g_defocus = gathered[:, COEF + orient_total + 1].astype(jnp.float32)
+    g_mask_all = meta[:, :orient_total]
+    g_alive = meta[:, orient_total] > 0.5
+    g_defocus = meta[:, orient_total + 1].astype(jnp.float32)
     mask = lax.dynamic_slice_in_dim(g_mask_all, zz * chip_orients, chip_orients, 1) > 0.5
 
     cosine = jnp.asarray(COSINE)
@@ -91,14 +90,13 @@
     ctf = -jnp.sin(jnp.pi * g_defocus[:, None] * radius[None, :] + 0.1)
     quad_half = (-0.5 * inv_noise * ctf * ctf).astype(jnp.bfloat16)
     ctf_half = (ctf * ctf).astype(jnp.bfloat16)
-    real_part = gathered[:, :COEF].astype(jnp.float32)
-    weighted_r = (inv_noise * ctf * real_part).astype(jnp.bfloat16)
+    noise_ctf = inv_noise * ctf
+    ctf, noise_ctf, quad_half, ctf_half = lax.optimization_barrier((ctf, noise_ctf, quad_half, ctf_half))
+    real_part = g_images[:, :COEF].astype(jnp.float32)
+    imag_part = g_images[:, COEF:].astype(jnp.float32)
+    weighted_r = (noise_ctf * real_part).astype(jnp.bfloat16)
+    weighted_i = (noise_ctf * imag_part).astype(jnp.bfloat16)
     image_r = (ctf * real_part).astype(jnp.bfloat16)
-    ctf, weighted_r, image_r, quad_half, ctf_half = lax.optimization_barrier(
-        (ctf, weighted_r, image_r, quad_half, ctf_half)
-    )
-    imag_part = g_imag.astype(jnp.float32)
-    weighted_i = (inv_noise * ctf * imag_part).astype(jnp.bfloat16)
     image_i = (ctf * imag_part).astype(jnp.bfloat16)
 
     slices_wide = local_slices.astype(jnp.float32)

time: 151 us -> 128 us (0.85)
  waiting for transfers between devices: 47.2 us -> 23.1 us
  starting transfers between devices: 17.9 us -> 26.2 us
  matrix products: 20.7 us -> 14.3 us
  local copies, waits for them, and re-layouts: 6.36 us -> 11.2 us
  other arithmetic: 38.9 us -> 35.8 us
  blocking collectives: 5.04 us -> 2.8 us
    all_gather x2 -> x1, waiting for transfers between devices: 29 us -> 6.23 us  [shards(): g_images = lax.all_gather(images, 'zz', axis=0, tiled=True)]
    all_to_all x1 -> x2, starting transfers between devices: 4.46 us -> 12.8 us  [exchange(): return lax.all_to_all(spread, axis, 0, 0, tiled=True)]
    unnamed x11 -> x25, local copies, waits for them, and re-layouts: 0.6 us -> 7.16 us
    dot_general x1, matrix products: 5.87 us -> 2.81 us  [shards(): lax.dot_general(weighted_i, parts_i, (((1,), (1,)), ((), ())), preferred_...]
    convert_element_type x2 -> x1, other arithmetic: 7.96 us -> 5.44 us  [split3(): second = rest.astype(jnp.bfloat16)]
    all_gather x1, blocking collectives: 5.04 us -> 2.8 us  [shards(): local_slices = lax.all_gather(slices, 'cc', axis=0, tiled=True)]
    convert_element_type x1, other arithmetic: 10.6 us -> 8.5 us  [shards(): ctf_half = (ctf * ctf).astype(jnp.bfloat16)]
    convert_element_type x1, other arithmetic: 1.43 us -> 3.51 us  [shards(): image_r = (ctf * real_part).astype(jnp.bfloat16)]
  transfers between devices with their start and end apart: 4 -> 4, of which waited for: 4 -> 3; matrix products, arithmetic and copies ran while one was open for 29% -> 24% of each run, Pallas kernels for 0% -> 0%
where the time goes in v4:
time: 128 us
  other arithmetic  35.8 us (28%)
  starting transfers between devices  26.2 us (20%)
  waiting for transfers between devices  23.1 us (18%)
  matrix products  14.3 us (11%)
  between operations  14.3 us (11%)
  local copies, waits for them, and re-layouts  11.2 us (9%)
  blocking collectives  2.8 us (2%)
    all_to_all x1, starting transfers between devices, shards(): lax.all_to_all(both, ('cc', 'dom'), 0, 0, tiled=True)  13.4 us
    all_to_all x1, waiting for transfers between devices, shards(): lax.all_to_all(both, ('cc', 'dom'), 0, 0, tiled=True)  13.2 us
    all_to_all x2, starting transfers between devices, exchange(): return lax.all_to_all(spread, axis, 0, 0, tiled=True)  12.8 us
    convert_element_type x1, other arithmetic, split3(): first = values.astype(jnp.bfloat16)  8.56 us
    convert_element_type x1, other arithmetic, shards(): ctf_half = (ctf * ctf).astype(jnp.bfloat16)  8.5 us
    unnamed x25, local copies, waits for them, and re-layouts  7.16 us
    dot_general x1, matrix products, shards(): lax.dot_general(weighted_r, parts_r, (((1,), (1,)), ((), ())), preferred_...  6.38 us
    all_gather x1, waiting for transfers between devices, shards(): g_images = lax.all_gather(images, 'zz', axis=0, tiled=True)  6.23 us
  transfers between devices with their start and end apart: 4, of which 3 were waited for; matrix products, arithmetic and copies ran while one was open for 24% of the time, Pallas kernels for 0%

profile of v4, /device:TPU:1, one launch (start us, length us, event | category | flops | bytes accessed | tf_op | source)
XLA Modules:
  0.0 127.7 jit_solution(6087554698235138514)
XLA Ops:
  7.8 0.7 iota_compare_fusion.1
  8.6 0.7 copy.30
  9.4 0.9 fusion.34
  11.1 9.0 %all-to-all-start = ((bf16[8,16,256]{2,1,0:T(8,128)(2,1)}), bf16[8,16,256]{2,1,0:T(8,128)(2,1)S(1)}, u32[]{:S(2)}, u32[]{:S(2)}) async-start(bf16[8,16,256]{2,1,0:T(8,128)(2,1)} %broadcast_in_dim.91), calls=%async_computation | async-start | bytes 131072 | tf_op jit(solution)/shard_map/all_to_all | solution.py:50
  20.2 0.7 all-gather.2.cloned.1.call-update
  20.9 2.8 %all_gather.7 = bf16[16,8192]{1,0:T(8,128)(2,1)S(1)} all-gather(bf16[8,8192]{1,0:T(8,128)(2,1)} %param.12), channel_id=1, replica_groups=mesh['dom'=16,'zz'=8,'cc'=2] {'cc'}, dimensions={0}, use_global_device_ids=true | all-gather | bytes 393216 | tf_op jit(solution)/shard_map/all_gather | solution.py:78
  23.8 3.0 %multiply_subtract_fusion = (f32[25,16,4096]{2,1,0:T(8,128)S(1)}, f32[25,16,4096]{2,1,0:T(8,128)S(1)}) fusion(f32[16,4096]{1,0:T(8,128)S(1)} %get-tuple-element.25, f32[25,4096]{1,0:T(8,128)} %constant.17.clone, f32[16,4096]{1,0:T(8,128)S(1)} %get-tuple-element.24, f32[25,4096]{1,0:T(8,128)} %constant.16.clone), kind=kLoop, calls=%fused_computation.20 | loop fusion | flops 9830400 | bytes 14450688 | tf_op jit(solution)/shard_map/sub | solution.py:116
  26.8 2.7 %copy-done = f32[25,16,4096]{2,1,0:T(8,128)} copy-done((f32[25,16,4096]{2,1,0:T(8,128)}, f32[25,16,4096]{2,1,0:T(8,128)S(1)}, u32[]{:S(2)}) %copy-start) | copy-done | bytes 6553624
  29.5 1.9 %copy-done.1 = f32[25,16,4096]{2,1,0:T(8,128)} copy-done((f32[25,16,4096]{2,1,0:T(8,128)}, f32[25,16,4096]{2,1,0:T(8,128)S(1)}, u32[]{:S(2)}) %copy-start.1) | copy-done | bytes 6553624
  31.4 5.4 %fusion.12 = (bf16[400,4096]{1,0:T(8,128)(2,1)}, bf16[400,4096]{1,0:T(8,128)(2,1)}, bf16[400,4096]{1,0:T(8,128)(2,1)}, bf16[400,4096]{1,0:T(8,128)(2,1)}) fusion(f32[25,16,4096]{2,1,0:T(8,128)S(1)} %get-tuple-element.23, f32[25,16,4096]{2,1,0:T(8,128)S(1)} %get-tuple-element.22), kind=kLoop, calls=%fused_computation.23 | loop fusion | flops 22937600 | bytes 26214400 | tf_op jit(solution)/shard_map/convert_element_type | solution.py:43
  36.8 8.6 %bitcast_convert_fusion = (bf16[400,4096]{1,0:T(8,128)(2,1)}, bf16[400,4096]{1,0:T(8,128)(2,1)}) fusion(f32[25,16,4096]{2,1,0:T(8,128)} %copy-done, f32[25,16,4096]{2,1,0:T(8,128)} %copy-done.1), kind=kLoop, calls=%fused_computation.14 | loop fusion | flops 3276800 | bytes 19660800 | tf_op jit(solution)/shard_map/convert_element_type | solution.py:41
  45.6 8.5 %multiply_convert_fusion = (bf16[128,4096]{1,0:T(8,128)(2,1)}, bf16[128,4096]{1,0:T(8,128)(2,1)S(1)}, f32[128,4096]{1,0:T(8,128)}, f32[128,4096]{1,0:T(8,128)S(1)}) fusion(f32[4096]{0:T(1024)S(1)} %copy-done.11, f32[128]{0:T(128)S(1)} %multiply_reduce_fusion, f32[4096]{0:T(1024)S(1)} %broadcast_multiply_fusion, f32[4096]{0:T(1024)S(1)} %copy-done.10), kind=kLoop, calls=%fused_computation.42 | loop fusion | flops 4718592 | bytes 6341120 | tf_op jit(solution)/shard_map/convert_element_type | solution.py:92
  55.2 6.2 %all-gather.2.cloned.1.call-done = bf16[128,8192]{1,0:T(8,128)(2,1)} async-done(((bf16[16,8192]{1,0:T(8,128)(2,1)}), bf16[128,8192]{1,0:T(8,128)(2,1)}) %all-gather.2.cloned.1.call-update) | async-done | bytes 2097168 | tf_op jit(solution)/shard_map/all_gather | solution.py:77
  61.4 6.4 %fusion = f32[128,1200]{0,1:T(8,128)S(1)} fusion(bf16[400,4096]{1,0:T(8,128)(2,1)} %get-tuple-element.19, bf16[400,4096]{1,0:T(8,128)(2,1)} %get-tuple-element.18, bf16[400,4096]{1,0:T(8,128)(2,1)} %get-tuple-element.36, f32[128,4096]{1,0:T(8,128)} %get-tuple-element.7, bf16[128,8192]{1,0:T(8,128)(2,1)} %all-gather.2.cloned.1.call-done), kind=kOutput, calls=%fused_computation | convolution fusion | flops 1289355264 | bytes 13590528 | tf_op jit(solution)/shard_map/dot_general | solution.py:119
  68.1 0.9 copy-done.5
  70.2 2.8 %fusion.19 = f32[128,1200]{0,1:T(8,128)S(1)} fusion(f32[128,1200]{0,1:T(8,128)S(1)} %fusion, bf16[400,4096]{1,0:T(8,128)(2,1)S(1)} %copy-done.3, bf16[400,4096]{1,0:T(8,128)(2,1)S(1)} %copy-done.4, bf16[400,4096]{1,0:T(8,128)(2,1)S(1)} %copy-done.5, f32[128,4096]{1,0:T(8,128)S(1)} %copy-done.7, bf16[128,8192]{1,0:T(8,128)(2,1)S(1)} %copy-done.6), kind=kOutput, calls=%fused_computation.36 | convolution fusion | flops 1289508864 | bytes 14204928 | tf_op jit(solution)/shard_map/dot_general | solution.py:121
  73.8 3.8 %all-to-all-start.1 = ((f32[8,2,128]{2,1,0:T(2,128)}), f32[8,2,128]{2,1,0:T(2,128)S(1)}, u32[]{:S(2)}, u32[]{:S(2)}) async-start(f32[8,2,128]{2,1,0:T(2,128)} %broadcast_in_dim.96), calls=%async_computation.1 | async-start | bytes 16384 | tf_op jit(solution)/shard_map/all_to_all | solution.py:50
  77.6 3.5 %fusion.23 = (bf16[128,4096]{1,0:T(8,128)(2,1)}, bf16[128,4096]{1,0:T(8,128)(2,1)}) fusion(f32[128,4096]{1,0:T(8,128)S(1)} %get-tuple-element.9, bf16[128,8192]{1,0:T(8,128)(2,1)} %all-gather.2.cloned.1.call-done), kind=kLoop, calls=%fused_computation.38 | loop fusion | flops 3145728 | bytes 6291456 | tf_op jit(solution)/shard_map/convert_element_type | solution.py:99
  81.1 3.1 %all-to-all-done.1 = f32[8,2,128]{2,1,0:T(2,128)S(1)} async-done(((f32[8,2,128]{2,1,0:T(2,128)}), f32[8,2,128]{2,1,0:T(2,128)S(1)}, u32[]{:S(2)}, u32[]{:S(2)}) %all-to-all-start.1) | async-done | bytes 8224 | tf_op jit(solution)/shard_map/all_to_all | solution.py:50
  84.3 4.3 %fusion.14 = f32[25,16,12288]{2,1,0:T(8,128)S(1)} fusion(bf16[25,16,128]{2,1,0:T(8,128)(2,1)S(1)} %bitcast.71, bf16[128,4096]{1,0:T(8,128)(2,1)S(1)} %copy-done.2, bf16[128,4096]{1,0:T(8,128)(2,1)} %get-tuple-element.21, bf16[128,4096]{1,0:T(8,128)(2,1)} %get-tuple-element.20), kind=kOutput, calls=%fused_computation.26 | convolution fusion | flops 1267728384 | bytes 22908928 | tf_op jit(solution)/shard_map/dot_general | solution.py:144
  88.7 2.8 %subtract_reduce_fusion = (f32[16,4096]{1,0:T(8,128)S(1)}, f32[16,4096]{1,0:T(8,128)S(1)}, f32[16,4096]{1,0:T(8,128)S(1)}) fusion(f32[25,16,12288]{2,1,0:T(8,128)S(1)} %fusion.14, f32[25,4096]{1,0:T(8,128)S(1)} %copy-done.8, f32[25,4096]{1,0:T(8,128)S(1)} %copy-done.9), kind=kLoop, calls=%fused_computation.18 | loop fusion | flops 14548992 | bytes 21266432 | tf_op jit(solution)/shard_map/reduce_sum | solution.py:153
  91.5 0.9 pad_maximum_fusion
  92.4 13.4 %all-to-all-start.2 = ((f32[32,8,768]{2,1,0:T(8,128)}), f32[32,8,768]{2,1,0:T(8,128)S(1)}, u32[]{:S(2)}, u32[]{:S(2)}) async-start(f32[32,8,768]{2,1,0:T(8,128)} %bitcast.19), calls=%async_computation.2 | async-start | bytes 1572864 | tf_op jit(solution)/shard_map/all_to_all | solution.py:169
  106.4 13.2 %all-to-all-done.2 = f32[32,8,768]{2,1,0:T(8,128)S(1)} async-done(((f32[32,8,768]{2,1,0:T(8,128)}), f32[32,8,768]{2,1,0:T(8,128)S(1)}, u32[]{:S(2)}, u32[]{:S(2)}) %all-to-all-start.2) | async-done | bytes 786464 | tf_op jit(solution)/shard_map/all_to_all | solution.py:169
  (55 shorter events, 7.2 us)
Async XLA Ops:
  11.1 34.3 %all-to-all-start = ((bf16[8,16,256]{2,1,0:T(8,128)(2,1)}), bf16[8,16,256]{2,1,0:T(8,128)(2,1)S(1)}, u32[]{:S(2)}, u32[]{:S(2)}) async-start(bf16[8,16,256]{2,1,0:T(8,128)(2,1)} %broadcast_in_dim.91), calls=%async_computation | async-start | bytes 131072 | tf_op jit(solution)/shard_map/all_to_all | solution.py:50
  20.1 41.3 %all-gather.2.cloned.1.call-start = ((), (), s32[]{:S(2)}) async-start(), calls=%async_computation.3 | async-start | bytes 2359296 | tf_op jit(solution)/shard_map/all_gather | solution.py:77
  26.7 2.7 %copy-start = (f32[25,16,4096]{2,1,0:T(8,128)}, f32[25,16,4096]{2,1,0:T(8,128)S(1)}, u32[]{:S(2)}) copy-start(f32[25,16,4096]{2,1,0:T(8,128)S(1)} %get-tuple-element.22) | copy-start | bytes 19660804
  26.7 4.7 %copy-start.1 = (f32[25,16,4096]{2,1,0:T(8,128)}, f32[25,16,4096]{2,1,0:T(8,128)S(1)}, u32[]{:S(2)}) copy-start(f32[25,16,4096]{2,1,0:T(8,128)S(1)} %get-tuple-element.23) | copy-start | bytes 19660804
  36.8 8.6 %copy-start.10 = (f32[4096]{0:T(1024)S(1)}, f32[4096]{0:T(1024)}, u32[]{:S(2)}) copy-start(f32[4096]{0:T(1024)} %param.11) | copy-start | bytes 49156
  36.8 8.8 %copy-start.11 = (f32[4096]{0:T(1024)S(1)}, f32[4096]{0:T(1024)}, u32[]{:S(2)}) copy-start(f32[4096]{0:T(1024)} %constant.44.clone) | copy-start | bytes 49156
  61.4 6.4 %copy-start.3 = (bf16[400,4096]{1,0:T(8,128)(2,1)S(1)}, bf16[400,4096]{1,0:T(8,128)(2,1)}, u32[]{:S(2)}) copy-start(bf16[400,4096]{1,0:T(8,128)(2,1)} %get-tuple-element.37) | copy-start | bytes 9830404
  61.4 6.7 %copy-start.4 = (bf16[400,4096]{1,0:T(8,128)(2,1)S(1)}, bf16[400,4096]{1,0:T(8,128)(2,1)}, u32[]{:S(2)}) copy-start(bf16[400,4096]{1,0:T(8,128)(2,1)} %get-tuple-element.38) | copy-start | bytes 9830404
  61.4 7.6 %copy-start.5 = (bf16[400,4096]{1,0:T(8,128)(2,1)S(1)}, bf16[400,4096]{1,0:T(8,128)(2,1)}, u32[]{:S(2)}) copy-start(bf16[400,4096]{1,0:T(8,128)(2,1)} %get-tuple-element.35) | copy-start | bytes 9830404
  61.4 8.2 %copy-start.6 = (bf16[128,8192]{1,0:T(8,128)(2,1)S(1)}, bf16[128,8192]{1,0:T(8,128)(2,1)}, u32[]{:S(2)}) copy-start(bf16[128,8192]{1,0:T(8,128)(2,1)} %all-gather.2.cloned.1.call-done) | copy-start | bytes 6291460
  61.4 8.8 %copy-start.7 = (f32[128,4096]{1,0:T(8,128)S(1)}, f32[128,4096]{1,0:T(8,128)}, u32[]{:S(2)}) copy-start(f32[128,4096]{1,0:T(8,128)} %get-tuple-element.7) | copy-start | bytes 6291460
  73.8 10.3 %all-to-all-start.1 = ((f32[8,2,128]{2,1,0:T(2,128)}), f32[8,2,128]{2,1,0:T(2,128)S(1)}, u32[]{:S(2)}, u32[]{:S(2)}) async-start(f32[8,2,128]{2,1,0:T(2,128)} %broadcast_in_dim.96), calls=%async_computation.1 | async-start | bytes 16384 | tf_op jit(solution)/shard_map/all_to_all | solution.py:50
  77.6 6.7 %copy-start.2 = (bf16[128,4096]{1,0:T(8,128)(2,1)S(1)}, bf16[128,4096]{1,0:T(8,128)(2,1)}, u32[]{:S(2)}) copy-start(bf16[128,4096]{1,0:T(8,128)(2,1)} %get-tuple-element.10) | copy-start | bytes 3145732
  84.3 4.4 %copy-start.8 = (f32[25,4096]{1,0:T(8,128)S(1)}, f32[25,4096]{1,0:T(8,128)}, u32[]{:S(2)}) copy-start(f32[25,4096]{1,0:T(8,128)} %constant.17.clone) | copy-start | bytes 1228804
  84.3 4.4 %copy-start.9 = (f32[25,4096]{1,0:T(8,128)S(1)}, f32[25,4096]{1,0:T(8,128)}, u32[]{:S(2)}) copy-start(f32[25,4096]{1,0:T(8,128)} %constant.16.clone) | copy-start | bytes 1228804
  92.4 27.1 %all-to-all-start.2 = ((f32[32,8,768]{2,1,0:T(8,128)}), f32[32,8,768]{2,1,0:T(8,128)S(1)}, u32[]{:S(2)}, u32[]{:S(2)}) async-start(f32[32,8,768]{2,1,0:T(8,128)} %bitcast.19), calls=%async_computation.2 | async-start | bytes 1572864 | tf_op jit(solution)/shard_map/all_to_all | solution.py:169
Sparse Core Ops, SparseCore 0:
  22.7 38.6 all-gather.1

commit v5 on v4

--- a/solution.py
+++ b/solution.py
@@ -45,6 +45,20 @@
     return first, second, third
 
 
+def ring_blocks(values, axis, size):
+    ahead = values
+    behind = values
+    later = []
+    sooner = [values]
+    for step in range(size // 2):
+        ahead = lax.ppermute(ahead, axis, [(i, (i + 1) % size) for i in range(size)])
+        later.append(ahead)
+        if step < (size - 1) // 2:
+            behind = lax.ppermute(behind, axis, [(i, (i - 1) % size) for i in range(size)])
+            sooner.append(behind)
+    return sooner + later[::-1]
+
+
 def exchange(values, axis, size):
     spread = jnp.broadcast_to(values[None], (size,) + values.shape)
     return lax.all_to_all(spread, axis, 0, 0, tiled=True)
@@ -73,10 +87,12 @@
         axis=1,
     )
     group = lax.axis_size("zz")
+    shift = zz * rows
     meta = exchange(extra, "zz", group).reshape(group * rows, extra.shape[1])
-    g_images = lax.all_gather(images, "zz", axis=0, tiled=True)
+    meta = jnp.roll(meta, -shift, axis=0)
+    blocks = ring_blocks(images, "zz", group)
     local_slices = lax.all_gather(slices, "cc", axis=0, tiled=True)
-    count = g_images.shape[0]
+    count = rows * group
     chip_orients = local_slices.shape[0]
 
     g_mask_all = meta[:, :orient_total]
@@ -92,8 +108,8 @@
     ctf_half = (ctf * ctf).astype(jnp.bfloat16)
     noise_ctf = inv_noise * ctf
     ctf, noise_ctf, quad_half, ctf_half = lax.optimization_barrier((ctf, noise_ctf, quad_half, ctf_half))
-    real_part = g_images[:, :COEF].astype(jnp.float32)
-    imag_part = g_images[:, COEF:].astype(jnp.float32)
+    real_part = jnp.concatenate([b[:, :COEF] for b in blocks], axis=0).astype(jnp.float32)
+    imag_part = jnp.concatenate([b[:, COEF:] for b in blocks], axis=0).astype(jnp.float32)
     weighted_r = (noise_ctf * real_part).astype(jnp.bfloat16)
     weighted_i = (noise_ctf * imag_part).astype(jnp.bfloat16)
     image_r = (ctf * real_part).astype(jnp.bfloat16)
@@ -129,16 +145,17 @@
     local_sum = jnp.sum(
         jnp.where(mask[:, None, :], jnp.exp(score - local_max[:, None, None]), 0.0), axis=(1, 2)
     )
-    stats = exchange(jnp.stack((local_max, local_sum)), "zz", group)
-    highest = jnp.max(stats[:, 0], axis=0)
-    normalizer = jnp.sum(stats[:, 1] * jnp.exp(stats[:, 0] - highest[None, :]), axis=0)
+    stats = exchange(jnp.roll(jnp.stack((local_max, local_sum)), shift, axis=1), "zz", group)
+    top = jnp.max(stats[:, 0], axis=0)
+    normalizer = jnp.roll(jnp.sum(stats[:, 1] * jnp.exp(stats[:, 0] - top[None, :]), axis=0), -shift)
+    highest = jnp.roll(top, -shift)
     highest = jnp.where(g_alive, highest, 0.0)
     normalizer = jnp.where(g_alive, normalizer, 1.0)
     expo = jnp.where(mask[:, None, :], jnp.exp(score - highest[:, None, None]), 0.0)
     posterior = (expo / normalizer[:, None, None]).astype(jnp.bfloat16)
     posterior = jnp.where(g_alive[:, None, None], posterior, jnp.zeros_like(posterior))
     peak_all = jnp.where(g_alive, 1.0 / normalizer, 0.0)
-    peak_weight = lax.dynamic_slice_in_dim(peak_all, zz * rows, rows, 0)
+    peak_weight = peak_all[:rows]
 
     flat_post = posterior.reshape(count, block)
     accum = lax.dot_general(
@@ -166,7 +183,8 @@
     )
     pieces = halves * doms
     both = both.reshape(pieces, own_orients, data_cols + weight_cols)
-    reduced = jnp.sum(lax.all_to_all(both, ("cc", "dom"), 0, 0, tiled=True), axis=0)
+    moved = lax.all_to_all(both.astype(jnp.bfloat16), ("cc", "dom"), 0, 0, tiled=True)
+    reduced = jnp.sum(moved.astype(jnp.float32), axis=0)
     data_out = reduced[:, :data_cols]
     weight_out = reduced[:, data_cols:]
     return (peak_weight, data_out, weight_out)

time: 128 us -> 127 us (level)
  blocking collectives: 2.8 us -> 25.2 us
  between operations: 14.3 us -> 0.94 us
  starting transfers between devices: 26.2 us -> 21.3 us
  other arithmetic: 35.8 us -> 31.5 us
  waiting for transfers between devices: 23.1 us -> 21.8 us
    all_to_all x0 -> x1, blocking collectives: none -> 21.9 us  [shards(): lax.all_to_all(both.astype(jnp.bfloat16), ('cc', 'dom'), 0, 0, tiled=True)]
    ppermute x0 -> x7, waiting for transfers between devices: none -> 18.6 us  [the longest x4 14 us: ring_blocks(): lax.ppermute(ahead, axis, [(i, (i + 1) % size) for i in range(size)])]
    all_to_all x1 -> x0, starting transfers between devices: 13.4 us -> none  [shards(): lax.all_to_all(both, ('cc', 'dom'), 0, 0, tiled=True)]
    all_to_all x1 -> x0, waiting for transfers between devices: 13.2 us -> none  [shards(): lax.all_to_all(both, ('cc', 'dom'), 0, 0, tiled=True)]
    ppermute x0 -> x7, starting transfers between devices: none -> 13 us  [the longest x3 13 us: ring_blocks(): lax.ppermute(behind, axis, [(i, (i - 1) % size) for i in range(size)])]
    all_gather x1 -> x0, waiting for transfers between devices: 6.23 us -> none  [shards(): g_images = lax.all_gather(images, 'zz', axis=0, tiled=True)]
    all_to_all x2, starting transfers between devices: 12.8 us -> 8.32 us  [exchange(): return lax.all_to_all(spread, axis, 0, 0, tiled=True)]
    dot_general x1, matrix products: 2.81 us -> 5.99 us  [shards(): lax.dot_general(weighted_i, parts_i, (((1,), (1,)), ((), ())), preferred_...]
  transfers between devices with their start and end apart: 4 -> 9, of which waited for: 3 -> 4; matrix products, arithmetic and copies ran while one was open for 24% -> 25% of each run, Pallas kernels for 0% -> 0%
where the time goes in v5:
time: 127 us; the launch traced here: 126 us
  other arithmetic  31.5 us (25%)
  blocking collectives  25.2 us (20%)
  waiting for transfers between devices  21.8 us (17%)
  starting transfers between devices  21.3 us (17%)
  matrix products  15.3 us (12%)
  local copies, waits for them, and re-layouts  10.4 us (8%)
    all_to_all x1, blocking collectives, shards(): lax.all_to_all(both.astype(jnp.bfloat16), ('cc', 'dom'), 0, 0, tiled=True)  21.9 us
    ppermute x4, waiting for transfers between devices, ring_blocks(): lax.ppermute(ahead, axis, [(i, (i + 1) % size) for i in range(size)])  14 us
    ppermute x3, starting transfers between devices, ring_blocks(): lax.ppermute(behind, axis, [(i, (i - 1) % size) for i in range(size)])  13 us
    all_to_all x2, starting transfers between devices, exchange(): return lax.all_to_all(spread, axis, 0, 0, tiled=True)  8.32 us
    convert_element_type x1, other arithmetic, shards(): ctf_half = (ctf * ctf).astype(jnp.bfloat16)  7.29 us
    convert_element_type x1, other arithmetic, split3(): first = values.astype(jnp.bfloat16)  6.51 us
    dot_general x1, matrix products, shards(): lax.dot_general(weighted_i, parts_i, (((1,), (1,)), ((), ())), preferred_...  5.99 us
    unnamed x37, local copies, waits for them, and re-layouts  5.86 us
  transfers between devices with their start and end apart: 9, of which 4 were waited for; matrix products, arithmetic and copies ran while one was open for 25% of the time, Pallas kernels for 0%

profile of v5, /device:TPU:1, one launch (start us, length us, event | category | flops | bytes accessed | tf_op | source)
XLA Modules:
  0.0 126.3 jit_solution(7837167122521967386)
XLA Ops:
  0.6 6.5 %collective-permute-start = (bf16[16,8192]{1,0:T(8,128)(2,1)}, bf16[16,8192]{1,0:T(8,128)(2,1)}, u32[]{:S(2)}, u32[]{:S(2)}) collective-permute-start(bf16[16,8192]{1,0:T(8,128)(2,1)} %param.11), channel_id=1, source_target_pairs={{0,14},{2,0},{4,2},{6,4},{8,6},{10,8},{12,10},{14,12},{1,15},{3,1}... | collective-permute-start | bytes 786440 | tf_op jit(solution)/shard_map/ppermute | solution.py:57
  11.1 4.1 %all-to-all-start = ((bf16[8,16,256]{2,1,0:T(8,128)(2,1)}), bf16[8,16,256]{2,1,0:T(8,128)(2,1)S(1)}, u32[]{:S(2)}, u32[]{:S(2)}) async-start(bf16[8,16,256]{2,1,0:T(8,128)(2,1)} %broadcast_in_dim.91), calls=%async_computation | async-start | bytes 131072 | tf_op jit(solution)/shard_map/all_to_all | solution.py:64
  15.1 3.3 %all_gather.3 = bf16[16,8192]{1,0:T(8,128)(2,1)S(1)} all-gather(bf16[8,8192]{1,0:T(8,128)(2,1)} %param.14), channel_id=1, replica_groups=mesh['dom'=16,'zz'=8,'cc'=2] {'cc'}, dimensions={0}, use_global_device_ids=true | all-gather | bytes 393216 | tf_op jit(solution)/shard_map/all_gather | solution.py:94
  18.6 2.4 %multiply_add_fusion = (f32[25,16,4096]{2,1,0:T(8,128)S(1)}, f32[25,16,4096]{2,1,0:T(8,128)S(1)}) fusion(f32[16,4096]{1,0:T(8,128)S(1)} %get-tuple-element.44, f32[25,4096]{1,0:T(8,128)} %constant.91.clone, f32[16,4096]{1,0:T(8,128)S(1)} %get-tuple-element.43, f32[25,4096]{1,0:T(8,128)} %constant.90.clone), kind=kLoop, calls=%fused_computation.22 | loop fusion | flops 9830400 | bytes 14450688 | tf_op jit(solution)/shard_map/add | solution.py:131
  21.0 2.7 %copy-done = f32[25,16,4096]{2,1,0:T(8,128)} copy-done((f32[25,16,4096]{2,1,0:T(8,128)}, f32[25,16,4096]{2,1,0:T(8,128)S(1)}, u32[]{:S(2)}) %copy-start) | copy-done | bytes 6553624
  23.7 5.4 %fusion.12 = (bf16[400,4096]{1,0:T(8,128)(2,1)}, bf16[400,4096]{1,0:T(8,128)(2,1)}, bf16[400,4096]{1,0:T(8,128)(2,1)}, bf16[400,4096]{1,0:T(8,128)(2,1)}) fusion(f32[25,16,4096]{2,1,0:T(8,128)S(1)} %get-tuple-element.25, f32[25,16,4096]{2,1,0:T(8,128)S(1)} %get-tuple-element.26), kind=kLoop, calls=%fused_computation.23 | loop fusion | flops 22937600 | bytes 26214400 | tf_op jit(solution)/shard_map/convert_element_type | solution.py:43
  29.2 6.5 %bitcast_convert_fusion = (bf16[400,4096]{1,0:T(8,128)(2,1)}, bf16[400,4096]{1,0:T(8,128)(2,1)}) fusion(f32[25,16,4096]{2,1,0:T(8,128)} %copy-done, f32[25,16,4096]{2,1,0:T(8,128)S(1)} %get-tuple-element.25), kind=kLoop, calls=%fused_computation.14 | loop fusion | flops 3276800 | bytes 19660800 | tf_op jit(solution)/shard_map/convert_element_type | solution.py:41
  36.8 7.3 %multiply_convert_fusion = (bf16[128,4096]{1,0:T(8,128)(2,1)S(1)}, bf16[128,4096]{1,0:T(8,128)(2,1)S(1)}, f32[128,4096]{1,0:T(8,128)S(1)}, f32[128,4096]{1,0:T(8,128)S(1)}) fusion(f32[4096]{0:T(1024)S(1)} %copy-done.14, f32[128]{0:T(128)S(1)} %fusion.47, f32[4096]{0:T(1024)S(1)} %broadcast_multiply_fusion, f32[4096]{0:T(1024)S(1)} %copy-done.13), kind=kLoop, calls=%fused_computation.42 | loop fusion | flops 4718592 | bytes 6341120 | tf_op jit(solution)/shard_map/convert_element_type | solution.py:108
  44.8 3.2 %collective-permute-start.1 = (bf16[16,8192]{1,0:T(8,128)(2,1)}, bf16[16,8192]{1,0:T(8,128)(2,1)S(1)}, u32[]{:S(2)}, u32[]{:S(2)}) collective-permute-start(bf16[16,8192]{1,0:T(8,128)(2,1)} %collective-permute-done), channel_id=1, source_target_pairs={{0,14},{2,0},{4,2},{6,4},{8,6},{10,8},{12,10},{14,12},{1,15},{3,1}... | collective-permute-start | bytes 786440 | tf_op jit(solution)/shard_map/ppermute | solution.py:57
  48.1 1.0 slice_dynamic-update-slice_fusion.13
  49.0 4.6 %collective-permute-done.1 = bf16[16,8192]{1,0:T(8,128)(2,1)S(1)} collective-permute-done((bf16[16,8192]{1,0:T(8,128)(2,1)}, bf16[16,8192]{1,0:T(8,128)(2,1)S(1)}, u32[]{:S(2)}, u32[]{:S(2)}) %collective-permute-start.1) | collective-permute-done | bytes 262176 | tf_op jit(solution)/shard_map/ppermute | solution.py:57
  53.6 3.3 %collective-permute-start.2 = (bf16[16,8192]{1,0:T(8,128)(2,1)S(1)}, bf16[16,8192]{1,0:T(8,128)(2,1)S(1)}, u32[]{:S(2)}, u32[]{:S(2)}) collective-permute-start(bf16[16,8192]{1,0:T(8,128)(2,1)S(1)} %collective-permute-done.1), channel_id=1, source_target_pairs={{0,14},{2,0},{4,2},{6,4},{8,6},{10,8},{12,10},{14,12},{1,15},{3,1}... | collective-permute-start | bytes 786440 | tf_op jit(solution)/shard_map/ppermute | solution.py:57
  57.0 7.5 %collective-permute-done.5 = bf16[16,8192]{1,0:T(8,128)(2,1)S(1)} collective-permute-done((bf16[16,8192]{1,0:T(8,128)(2,1)S(1)}, bf16[16,8192]{1,0:T(8,128)(2,1)S(1)}, u32[]{:S(2)}, u32[]{:S(2)}) %collective-permute-start.5) | collective-permute-done | bytes 262176 | tf_op jit(solution)/shard_map/ppermute | solution.py:54
  64.6 6.4 %collective-permute-done.6 = bf16[16,8192]{1,0:T(8,128)(2,1)S(1)} collective-permute-done((bf16[16,8192]{1,0:T(8,128)(2,1)S(1)}, bf16[16,8192]{1,0:T(8,128)(2,1)S(1)}, u32[]{:S(2)}, u32[]{:S(2)}) %collective-permute-start.6) | collective-permute-done | bytes 262176 | tf_op jit(solution)/shard_map/ppermute | solution.py:54
  71.0 1.0 slice_dynamic-update-slice_fusion.7
  72.1 1.0 copy-done.9
  73.4 6.0 %fusion.6 = f32[128,1200]{0,1:T(8,128)} fusion(bf16[400,4096]{1,0:T(8,128)(2,1)S(1)} %copy-done.4, bf16[400,4096]{1,0:T(8,128)(2,1)S(1)} %copy-done.5, bf16[400,4096]{1,0:T(8,128)(2,1)} %get-tuple-element.52, f32[128,4096]{1,0:T(8,128)S(1)} %get-tuple-element.8, bf16[128,4096]{1,0:T(8,128)(2,1)} %copy-done.11), kind=kOutput, calls=%fused_computation.6 | convolution fusion | flops 1289355264 | bytes 13590528 | tf_op jit(solution)/shard_map/dot_general | solution.py:137
  79.4 4.2 %fusion.19 = f32[128,1200]{0,1:T(8,128)S(1)} fusion(f32[128,1200]{0,1:T(8,128)} %fusion.6, bf16[400,4096]{1,0:T(8,128)(2,1)S(1)} %copy-done.2, bf16[400,4096]{1,0:T(8,128)(2,1)S(1)} %copy-done.1, bf16[400,4096]{1,0:T(8,128)(2,1)S(1)} %copy-done.3, f32[128,4096]{1,0:T(8,128)S(1)} %get-tuple-element.8, bf16[128,4096]{1,0:T(8,128)(2,1)} %copy-done.9), kind=kOutput, calls=%fused_computation.36 | convolution fusion | flops 1289508864 | bytes 14204928 | tf_op jit(solution)/shard_map/dot_general | solution.py:135
  84.4 4.2 %all-to-all-start.1 = ((f32[8,2,128]{2,1,0:T(2,128)}), f32[8,2,128]{2,1,0:T(2,128)S(1)}, u32[]{:S(2)}, u32[]{:S(2)}) async-start(f32[8,2,128]{2,1,0:T(2,128)} %broadcast_in_dim.96), calls=%async_computation.1 | async-start | bytes 16384 | tf_op jit(solution)/shard_map/all_to_all | solution.py:64
  88.6 3.4 %fusion.23 = (bf16[128,4096]{1,0:T(8,128)(2,1)}, bf16[128,4096]{1,0:T(8,128)(2,1)}) fusion(f32[128,4096]{1,0:T(8,128)S(1)} %get-tuple-element.10, bf16[128,4096]{1,0:T(8,128)(2,1)} %copy-done.9, bf16[128,4096]{1,0:T(8,128)(2,1)} %copy-done.11), kind=kLoop, calls=%fused_computation.38 | loop fusion | flops 3145728 | bytes 6291456 | tf_op jit(solution)/shard_map/convert_element_type | solution.py:115
  92.0 3.2 %all-to-all-done.1 = f32[8,2,128]{2,1,0:T(2,128)S(1)} async-done(((f32[8,2,128]{2,1,0:T(2,128)}), f32[8,2,128]{2,1,0:T(2,128)S(1)}, u32[]{:S(2)}, u32[]{:S(2)}) %all-to-all-start.1) | async-done | bytes 8224 | tf_op jit(solution)/shard_map/all_to_all | solution.py:64
  96.0 4.3 %fusion.14 = f32[25,16,12288]{2,1,0:T(8,128)S(1)} fusion(bf16[25,16,128]{2,1,0:T(8,128)(2,1)S(1)} %bitcast.84, bf16[128,4096]{1,0:T(8,128)(2,1)S(1)} %get-tuple-element.11, bf16[128,4096]{1,0:T(8,128)(2,1)} %get-tuple-element.24, bf16[128,4096]{1,0:T(8,128)(2,1)} %get-tuple-element.23), kind=kOutput, calls=%fused_computation.26 | convolution fusion | flops 1267728384 | bytes 22908928 | tf_op jit(solution)/shard_map/dot_general | solution.py:161
  100.3 2.8 %subtract_reduce_fusion = (bf16[16,4096]{1,0:T(8,128)(2,1)S(1)}, bf16[16,4096]{1,0:T(8,128)(2,1)S(1)}, bf16[16,4096]{1,0:T(8,128)(2,1)S(1)}) fusion(f32[25,16,12288]{2,1,0:T(8,128)S(1)} %fusion.14, f32[25,4096]{1,0:T(8,128)S(1)} %copy-done.6, f32[25,4096]{1,0:T(8,128)S(1)} %copy-done.7), kind=kLoop, calls=%fused_computation.18 | loop fusion | flops 14548992 | bytes 20873216 | tf_op jit(solution)/shard_map/reduce_sum | solution.py:170
  103.2 21.9 %all_to_all.15 = bf16[32,8,768]{2,1,0:T(8,128)(2,1)S(1)} all-to-all(bf16[32,8,768]{2,1,0:T(8,128)(2,1)S(1)} %bitcast.81), channel_id=1, replica_groups=mesh['dom'=16,'zz'=8,'cc'=2] {'cc','dom'}, dimensions={0} | all-to-all | bytes 786432 | tf_op jit(solution)/shard_map/all_to_all | solution.py:186
  (80 shorter events, 9.2 us)
Async XLA Ops:
  0.6 44.2 %collective-permute-start = (bf16[16,8192]{1,0:T(8,128)(2,1)}, bf16[16,8192]{1,0:T(8,128)(2,1)}, u32[]{:S(2)}, u32[]{:S(2)}) collective-permute-start(bf16[16,8192]{1,0:T(8,128)(2,1)} %param.11), channel_id=1, source_target_pairs={{0,14},{2,0},{4,2},{6,4},{8,6},{10,8},{12,10},{14,12},{1,15},{3,1}... | collective-permute-start | bytes 786440 | tf_op jit(solution)/shard_map/ppermute | solution.py:57
  7.1 40.9 %collective-permute-start.3 = (bf16[16,8192]{1,0:T(8,128)(2,1)}, bf16[16,8192]{1,0:T(8,128)(2,1)}, u32[]{:S(2)}, u32[]{:S(2)}) collective-permute-start(bf16[16,8192]{1,0:T(8,128)(2,1)} %param.11), channel_id=1, source_target_pairs={{0,2},{2,4},{4,6},{6,8},{8,10},{10,12},{12,14},{14,0},{1,3},{3,5},... | collective-permute-start | bytes 786440 | tf_op jit(solution)/shard_map/ppermute | solution.py:54
  11.1 25.3 %all-to-all-start = ((bf16[8,16,256]{2,1,0:T(8,128)(2,1)}), bf16[8,16,256]{2,1,0:T(8,128)(2,1)S(1)}, u32[]{:S(2)}, u32[]{:S(2)}) async-start(bf16[8,16,256]{2,1,0:T(8,128)(2,1)} %broadcast_in_dim.91), calls=%async_computation | async-start | bytes 131072 | tf_op jit(solution)/shard_map/all_to_all | solution.py:64
  21.0 2.7 %copy-start = (f32[25,16,4096]{2,1,0:T(8,128)}, f32[25,16,4096]{2,1,0:T(8,128)S(1)}, u32[]{:S(2)}) copy-start(f32[25,16,4096]{2,1,0:T(8,128)S(1)} %get-tuple-element.26) | copy-start | bytes 19660804
  29.2 6.5 %copy-start.12 = (bf16[16,8192]{1,0:T(8,128)(2,1)S(1)}, bf16[16,8192]{1,0:T(8,128)(2,1)}, u32[]{:S(2)}) copy-start(bf16[16,8192]{1,0:T(8,128)(2,1)} %param.11) | copy-start | bytes 786436
  29.2 7.2 %copy-start.13 = (f32[4096]{0:T(1024)S(1)}, f32[4096]{0:T(1024)}, u32[]{:S(2)}) copy-start(f32[4096]{0:T(1024)} %param.13) | copy-start | bytes 49156
  29.2 7.6 %copy-start.14 = (f32[4096]{0:T(1024)S(1)}, f32[4096]{0:T(1024)}, u32[]{:S(2)}) copy-start(f32[4096]{0:T(1024)} %constant.92.clone) | copy-start | bytes 49156
  36.5 11.5 %copy-start.8 = (bf16[128,4096]{1,0:T(8,128)(2,1)S(1)}, bf16[128,4096]{1,0:T(8,128)(2,1)}, u32[]{:S(2)}) copy-start(bf16[128,4096]{1,0:T(8,128)(2,1)} %get-tuple-element.41) | copy-start | bytes 3145732
  36.5 11.5 %copy-start.10 = (bf16[128,4096]{1,0:T(8,128)(2,1)S(1)}, bf16[128,4096]{1,0:T(8,128)(2,1)}, u32[]{:S(2)}) copy-start(bf16[128,4096]{1,0:T(8,128)(2,1)} %get-tuple-element.42) | copy-start | bytes 3145732
  36.6 36.8 %copy-start.4 = (bf16[400,4096]{1,0:T(8,128)(2,1)S(1)}, bf16[400,4096]{1,0:T(8,128)(2,1)}, u32[]{:S(2)}) copy-start(bf16[400,4096]{1,0:T(8,128)(2,1)} %get-tuple-element.54) | copy-start | bytes 9830404
  36.6 36.8 %copy-start.5 = (bf16[400,4096]{1,0:T(8,128)(2,1)S(1)}, bf16[400,4096]{1,0:T(8,128)(2,1)}, u32[]{:S(2)}) copy-start(bf16[400,4096]{1,0:T(8,128)(2,1)} %get-tuple-element.55) | copy-start | bytes 9830404
  44.8 8.8 %collective-permute-start.1 = (bf16[16,8192]{1,0:T(8,128)(2,1)}, bf16[16,8192]{1,0:T(8,128)(2,1)S(1)}, u32[]{:S(2)}, u32[]{:S(2)}) collective-permute-start(bf16[16,8192]{1,0:T(8,128)(2,1)} %collective-permute-done), channel_id=1, source_target_pairs={{0,14},{2,0},{4,2},{6,4},{8,6},{10,8},{12,10},{14,12},{1,15},{3,1}... | collective-permute-start | bytes 786440 | tf_op jit(solution)/shard_map/ppermute | solution.py:57
  48.0 8.9 %collective-permute-start.4 = (bf16[16,8192]{1,0:T(8,128)(2,1)}, bf16[16,8192]{1,0:T(8,128)(2,1)S(1)}, u32[]{:S(2)}, u32[]{:S(2)}) collective-permute-start(bf16[16,8192]{1,0:T(8,128)(2,1)} %collective-permute-done.3), channel_id=1, source_target_pairs={{0,2},{2,4},{4,6},{6,8},{8,10},{10,12},{12,14},{14,0},{1,3},{3,5},... | collective-permute-start | bytes 786440 | tf_op jit(solution)/shard_map/ppermute | solution.py:54
  53.6 10.9 %collective-permute-start.2 = (bf16[16,8192]{1,0:T(8,128)(2,1)S(1)}, bf16[16,8192]{1,0:T(8,128)(2,1)S(1)}, u32[]{:S(2)}, u32[]{:S(2)}) collective-permute-start(bf16[16,8192]{1,0:T(8,128)(2,1)S(1)} %collective-permute-done.1), channel_id=1, source_target_pairs={{0,14},{2,0},{4,2},{6,4},{8,6},{10,8},{12,10},{14,12},{1,15},{3,1}... | collective-permute-start | bytes 786440 | tf_op jit(solution)/shard_map/ppermute | solution.py:57
  57.0 7.6 %collective-permute-start.5 = (bf16[16,8192]{1,0:T(8,128)(2,1)S(1)}, bf16[16,8192]{1,0:T(8,128)(2,1)S(1)}, u32[]{:S(2)}, u32[]{:S(2)}) collective-permute-start(bf16[16,8192]{1,0:T(8,128)(2,1)S(1)} %collective-permute-done.4), channel_id=1, source_target_pairs={{0,2},{2,4},{4,6},{6,8},{8,10},{10,12},{12,14},{14,0},{1,3},{3,5},... | collective-permute-start | bytes 786440 | tf_op jit(solution)/shard_map/ppermute | solution.py:54
  64.5 6.4 %collective-permute-start.6 = (bf16[16,8192]{1,0:T(8,128)(2,1)S(1)}, bf16[16,8192]{1,0:T(8,128)(2,1)S(1)}, u32[]{:S(2)}, u32[]{:S(2)}) collective-permute-start(bf16[16,8192]{1,0:T(8,128)(2,1)S(1)} %collective-permute-done.5), channel_id=1, source_target_pairs={{0,2},{2,4},{4,6},{6,8},{8,10},{10,12},{12,14},{14,0},{1,3},{3,5},... | collective-permute-start | bytes 786440 | tf_op jit(solution)/shard_map/ppermute | solution.py:54
  72.0 1.0 copy-start.9
  72.0 1.3 %copy-start.11 = (bf16[128,4096]{1,0:T(8,128)(2,1)}, bf16[128,4096]{1,0:T(8,128)(2,1)S(1)}, u32[]{:S(2)}) copy-start(bf16[128,4096]{1,0:T(8,128)(2,1)S(1)} %get-tuple-element.28) | copy-start | bytes 3145732
  73.4 6.0 %copy-start.1 = (bf16[400,4096]{1,0:T(8,128)(2,1)S(1)}, bf16[400,4096]{1,0:T(8,128)(2,1)}, u32[]{:S(2)}) copy-start(bf16[400,4096]{1,0:T(8,128)(2,1)} %get-tuple-element.19) | copy-start | bytes 9830404
  73.4 6.0 %copy-start.2 = (bf16[400,4096]{1,0:T(8,128)(2,1)S(1)}, bf16[400,4096]{1,0:T(8,128)(2,1)}, u32[]{:S(2)}) copy-start(bf16[400,4096]{1,0:T(8,128)(2,1)} %get-tuple-element.20) | copy-start | bytes 9830404
  73.4 6.0 %copy-start.3 = (bf16[400,4096]{1,0:T(8,128)(2,1)S(1)}, bf16[400,4096]{1,0:T(8,128)(2,1)}, u32[]{:S(2)}) copy-start(bf16[400,4096]{1,0:T(8,128)(2,1)} %get-tuple-element.53) | copy-start | bytes 9830404
  84.4 10.8 %all-to-all-start.1 = ((f32[8,2,128]{2,1,0:T(2,128)}), f32[8,2,128]{2,1,0:T(2,128)S(1)}, u32[]{:S(2)}, u32[]{:S(2)}) async-start(f32[8,2,128]{2,1,0:T(2,128)} %broadcast_in_dim.96), calls=%async_computation.1 | async-start | bytes 16384 | tf_op jit(solution)/shard_map/all_to_all | solution.py:64
  96.0 4.4 %copy-start.6 = (f32[25,4096]{1,0:T(8,128)S(1)}, f32[25,4096]{1,0:T(8,128)}, u32[]{:S(2)}) copy-start(f32[25,4096]{1,0:T(8,128)} %constant.91.clone) | copy-start | bytes 1228804
  96.0 4.4 %copy-start.7 = (f32[25,4096]{1,0:T(8,128)S(1)}, f32[25,4096]{1,0:T(8,128)}, u32[]{:S(2)}) copy-start(f32[25,4096]{1,0:T(8,128)} %constant.90.clone) | copy-start | bytes 1228804

commit v6 on v5

--- a/solution.py
+++ b/solution.py
@@ -45,20 +45,6 @@
     return first, second, third
 
 
-def ring_blocks(values, axis, size):
-    ahead = values
-    behind = values
-    later = []
-    sooner = [values]
-    for step in range(size // 2):
-        ahead = lax.ppermute(ahead, axis, [(i, (i + 1) % size) for i in range(size)])
-        later.append(ahead)
-        if step < (size - 1) // 2:
-            behind = lax.ppermute(behind, axis, [(i, (i - 1) % size) for i in range(size)])
-            sooner.append(behind)
-    return sooner + later[::-1]
-
-
 def exchange(values, axis, size):
     spread = jnp.broadcast_to(values[None], (size,) + values.shape)
     return lax.all_to_all(spread, axis, 0, 0, tiled=True)
@@ -90,8 +76,19 @@
     shift = zz * rows
     meta = exchange(extra, "zz", group).reshape(group * rows, extra.shape[1])
     meta = jnp.roll(meta, -shift, axis=0)
-    blocks = ring_blocks(images, "zz", group)
     local_slices = lax.all_gather(slices, "cc", axis=0, tiled=True)
+    up = [(i, (i + 1) % group) for i in range(group)]
+    down = [(i, (i - 1) % group) for i in range(group)]
+    ahead1 = lax.ppermute(images, "zz", up)
+    behind1 = lax.ppermute(images, "zz", down)
+    ahead1, behind1, local_slices = lax.optimization_barrier((ahead1, behind1, local_slices))
+    ahead2 = lax.ppermute(ahead1, "zz", up)
+    behind2 = lax.ppermute(behind1, "zz", down)
+    ahead2, behind2, meta = lax.optimization_barrier((ahead2, behind2, meta))
+    ahead3 = lax.ppermute(ahead2, "zz", up)
+    behind3 = lax.ppermute(behind2, "zz", down)
+    ahead4 = lax.ppermute(ahead3, "zz", up)
+    blocks = [images, behind1, behind2, behind3, ahead4, ahead3, ahead2, ahead1]
     count = rows * group
     chip_orients = local_slices.shape[0]
 

time: 127 us -> 132 us (1.039)
  starting transfers between devices: 21.3 us -> 24.4 us
  local copies, waits for them, and re-layouts: 10.4 us -> 13 us
  waiting for transfers between devices: 21.8 us -> 19.5 us
    all_to_all x2, starting transfers between devices: 8.32 us -> 12.3 us  [exchange(): return lax.all_to_all(spread, axis, 0, 0, tiled=True)]
    ppermute x7, waiting for transfers between devices: 18.6 us -> 14.8 us  [the longest x1 6.85 us: shards(): ahead4 = lax.ppermute(ahead3, 'zz', up)]
    unnamed x37 -> x31, local copies, waits for them, and re-layouts: 5.86 us -> 8.78 us
    add x1 -> x0, other arithmetic: 2.44 us -> none  [shards(): turned_r = (c_t * s_real + s_t * s_imag).reshape(block, COEF)]
    sub x0 -> x1, other arithmetic: none -> 2.44 us  [shards(): turned_i = (c_t * s_imag - s_t * s_real).reshape(block, COEF)]
    dot_general x1, matrix products: 4.17 us -> 6.01 us  [shards(): lax.dot_general(weighted_r, parts_r, (((1,), (1,)), ((), ())), preferred_...]
    dot_general x1, matrix products: 5.99 us -> 4.17 us  [shards(): lax.dot_general(weighted_i, parts_i, (((1,), (1,)), ((), ())), preferred_...]
    all_to_all x2, waiting for transfers between devices: 3.19 us -> 4.64 us  [exchange(): return lax.all_to_all(spread, axis, 0, 0, tiled=True)]
  transfers between devices with their start and end apart: 9 -> 9, of which waited for: 4 -> 5; matrix products, arithmetic and copies ran while one was open for 25% -> 10% of each run, Pallas kernels for 0% -> 0%
where the time goes in v6:
time: 132 us; the launch traced here: 131 us
  other arithmetic  32.8 us (25%)
  blocking collectives  25.5 us (19%)
  starting transfers between devices  24.4 us (18%)
  waiting for transfers between devices  19.5 us (15%)
  matrix products  15.3 us (12%)
  local copies, waits for them, and re-layouts  13 us (10%)
    all_to_all x1, blocking collectives, shards(): lax.all_to_all(both.astype(jnp.bfloat16), ('cc', 'dom'), 0, 0, tiled=True)  22.1 us
    all_to_all x2, starting transfers between devices, exchange(): return lax.all_to_all(spread, axis, 0, 0, tiled=True)  12.3 us
    unnamed x31, local copies, waits for them, and re-layouts  8.78 us
    convert_element_type x1, other arithmetic, shards(): ctf_half = (ctf * ctf).astype(jnp.bfloat16)  7.29 us
    convert_element_type x1, other arithmetic, split3(): first = values.astype(jnp.bfloat16)  7.05 us
    ppermute x1, waiting for transfers between devices, shards(): ahead4 = lax.ppermute(ahead3, 'zz', up)  6.85 us
    dot_general x1, matrix products, shards(): lax.dot_general(weighted_r, parts_r, (((1,), (1,)), ((), ())), preferred_...  6.01 us
    convert_element_type x1, other arithmetic, split3(): second = rest.astype(jnp.bfloat16)  5.47 us
  transfers between devices with their start and end apart: 9, of which 5 were waited for; matrix products, arithmetic and copies ran while one was open for 10% of the time, Pallas kernels for 0%

profile of v6, /device:TPU:1, one launch (start us, length us, event | category | flops | bytes accessed | tf_op | source)
XLA Modules:
  0.0 131.2 jit_solution(13280149584753267863)
XLA Ops:
  0.6 2.5 %collective-permute-start = (bf16[16,8192]{1,0:T(8,128)(2,1)}, bf16[16,8192]{1,0:T(8,128)(2,1)S(1)}, u32[]{:S(2)}, u32[]{:S(2)}) collective-permute-start(bf16[16,8192]{1,0:T(8,128)(2,1)} %param.11), channel_id=1, source_target_pairs={{0,2},{2,4},{4,6},{6,8},{8,10},{10,12},{12,14},{14,0},{1,3},{3,5},... | collective-permute-start | bytes 786440 | tf_op jit(solution)/shard_map/ppermute | solution.py:82
  3.2 4.0 %collective-permute-start.1 = (bf16[16,8192]{1,0:T(8,128)(2,1)}, bf16[16,8192]{1,0:T(8,128)(2,1)S(1)}, u32[]{:S(2)}, u32[]{:S(2)}) collective-permute-start(bf16[16,8192]{1,0:T(8,128)(2,1)} %param.11), channel_id=1, source_target_pairs={{0,14},{2,0},{4,2},{6,4},{8,6},{10,8},{12,10},{14,12},{1,15},{3,1}... | collective-permute-start | bytes 786440 | tf_op jit(solution)/shard_map/ppermute | solution.py:83
  11.1 5.2 %all-to-all-start = ((bf16[8,16,256]{2,1,0:T(8,128)(2,1)}), bf16[8,16,256]{2,1,0:T(8,128)(2,1)S(1)}, u32[]{:S(2)}, u32[]{:S(2)}) async-start(bf16[8,16,256]{2,1,0:T(8,128)(2,1)} %broadcast_in_dim.91), calls=%async_computation | async-start | bytes 131072 | tf_op jit(solution)/shard_map/all_to_all | solution.py:50
  16.3 1.7 %slice_dynamic-update-slice_fusion.10 = (bf16[128,4096]{1,0:T(8,128)(2,1)}, bf16[128,4096]{1,0:T(8,128)(2,1)}) fusion(bf16[16,8192]{1,0:T(8,128)(2,1)} %param.11), kind=kLoop, calls=%fused_computation.78 | loop fusion | bytes 524288
  18.8 3.3 %all_gather.3 = bf16[16,8192]{1,0:T(8,128)(2,1)S(1)} all-gather(bf16[8,8192]{1,0:T(8,128)(2,1)} %param.14), channel_id=1, replica_groups=mesh['dom'=16,'zz'=8,'cc'=2] {'cc'}, dimensions={0}, use_global_device_ids=true | all-gather | bytes 393216 | tf_op jit(solution)/shard_map/all_gather | solution.py:79
  22.1 1.5 %all-to-all-done = bf16[8,16,256]{2,1,0:T(8,128)(2,1)S(1)} async-done(((bf16[8,16,256]{2,1,0:T(8,128)(2,1)}), bf16[8,16,256]{2,1,0:T(8,128)(2,1)S(1)}, u32[]{:S(2)}, u32[]{:S(2)}) %all-to-all-start) | async-done | bytes 65568 | tf_op jit(solution)/shard_map/all_to_all | solution.py:50
  23.9 2.4 %multiply_subtract_fusion = (f32[25,16,4096]{2,1,0:T(8,128)S(1)}, f32[25,16,4096]{2,1,0:T(8,128)S(1)}) fusion(f32[16,4096]{1,0:T(8,128)S(1)} %get-tuple-element.56, f32[25,4096]{1,0:T(8,128)} %constant.91.clone, f32[16,4096]{1,0:T(8,128)S(1)} %get-tuple-element.55, f32[25,4096]{1,0:T(8,128)} %constant.90.clone), kind=kLoop, calls=%fused_computation.20 | loop fusion | flops 9830400 | bytes 14450688 | tf_op jit(solution)/shard_map/sub | solution.py:129
  26.4 2.7 %copy-done = f32[25,16,4096]{2,1,0:T(8,128)} copy-done((f32[25,16,4096]{2,1,0:T(8,128)}, f32[25,16,4096]{2,1,0:T(8,128)S(1)}, u32[]{:S(2)}) %copy-start) | copy-done | bytes 6553624
  29.1 5.5 %fusion.12 = (bf16[400,4096]{1,0:T(8,128)(2,1)}, bf16[400,4096]{1,0:T(8,128)(2,1)}, bf16[400,4096]{1,0:T(8,128)(2,1)}, bf16[400,4096]{1,0:T(8,128)(2,1)}) fusion(f32[25,16,4096]{2,1,0:T(8,128)S(1)} %get-tuple-element.38, f32[25,16,4096]{2,1,0:T(8,128)S(1)} %get-tuple-element.37), kind=kLoop, calls=%fused_computation.23 | loop fusion | flops 22937600 | bytes 26214400 | tf_op jit(solution)/shard_map/convert_element_type | solution.py:43
  34.6 7.0 %bitcast_convert_fusion = (bf16[400,4096]{1,0:T(8,128)(2,1)}, bf16[400,4096]{1,0:T(8,128)(2,1)}) fusion(f32[25,16,4096]{2,1,0:T(8,128)S(1)} %get-tuple-element.37, f32[25,16,4096]{2,1,0:T(8,128)} %copy-done), kind=kLoop, calls=%fused_computation.14 | loop fusion | flops 3276800 | bytes 19660800 | tf_op jit(solution)/shard_map/convert_element_type | solution.py:41
  41.9 2.4 %collective-permute-start.3 = (bf16[16,8192]{1,0:T(8,128)(2,1)S(1)}, bf16[16,8192]{1,0:T(8,128)(2,1)S(1)}, u32[]{:S(2)}, u32[]{:S(2)}) collective-permute-start(bf16[16,8192]{1,0:T(8,128)(2,1)S(1)} %collective-permute-done.1), channel_id=1, source_target_pairs={{0,14},{2,0},{4,2},{6,4},{8,6},{10,8},{12,10},{14,12},{1,15},{3,1}... | collective-permute-start | bytes 786440 | tf_op jit(solution)/shard_map/ppermute | solution.py:86
  45.0 3.0 %collective-permute-done.2 = bf16[16,8192]{1,0:T(8,128)(2,1)S(1)} collective-permute-done((bf16[16,8192]{1,0:T(8,128)(2,1)S(1)}, bf16[16,8192]{1,0:T(8,128)(2,1)S(1)}, u32[]{:S(2)}, u32[]{:S(2)}) %collective-permute-start.2) | collective-permute-done | bytes 262176 | tf_op jit(solution)/shard_map/ppermute | solution.py:85
  48.1 7.3 %multiply_convert_fusion = (bf16[128,4096]{1,0:T(8,128)(2,1)S(1)}, bf16[128,4096]{1,0:T(8,128)(2,1)S(1)}, f32[128,4096]{1,0:T(8,128)S(1)}, f32[128,4096]{1,0:T(8,128)S(1)}) fusion(f32[4096]{0:T(1024)S(1)} %copy-done.11, f32[128]{0:T(128)S(1)} %multiply_bitcast_fusion, f32[4096]{0:T(1024)S(1)} %broadcast_multiply_fusion, f32[4096]{0:T(1024)S(1)} %copy-done.10), kind=kLoop, calls=%fused_computation.42 | loop fusion | flops 4718592 | bytes 6341120 | tf_op jit(solution)/shard_map/convert_element_type | solution.py:105
  55.4 2.7 %collective-permute-start.4 = (bf16[16,8192]{1,0:T(8,128)(2,1)S(1)}, bf16[16,8192]{1,0:T(8,128)(2,1)S(1)}, u32[]{:S(2)}, u32[]{:S(2)}) collective-permute-start(bf16[16,8192]{1,0:T(8,128)(2,1)S(1)} %collective-permute-done.3), channel_id=1, source_target_pairs={{0,14},{2,0},{4,2},{6,4},{8,6},{10,8},{12,10},{14,12},{1,15},{3,1}... | collective-permute-start | bytes 786440 | tf_op jit(solution)/shard_map/ppermute | solution.py:89
  59.7 4.9 %collective-permute-done.5 = bf16[16,8192]{1,0:T(8,128)(2,1)S(1)} collective-permute-done((bf16[16,8192]{1,0:T(8,128)(2,1)S(1)}, bf16[16,8192]{1,0:T(8,128)(2,1)S(1)}, u32[]{:S(2)}, u32[]{:S(2)}) %collective-permute-start.5) | collective-permute-done | bytes 262176 | tf_op jit(solution)/shard_map/ppermute | solution.py:88
  65.4 6.8 %collective-permute-done.6 = bf16[16,8192]{1,0:T(8,128)(2,1)S(1)} collective-permute-done((bf16[16,8192]{1,0:T(8,128)(2,1)S(1)}, bf16[16,8192]{1,0:T(8,128)(2,1)S(1)}, u32[]{:S(2)}, u32[]{:S(2)}) %collective-permute-start.6) | collective-permute-done | bytes 262176 | tf_op jit(solution)/shard_map/ppermute | solution.py:90
  75.1 6.0 %fusion = f32[128,1200]{0,1:T(8,128)} fusion(bf16[400,4096]{1,0:T(8,128)(2,1)S(1)} %copy-done.5, bf16[400,4096]{1,0:T(8,128)(2,1)S(1)} %copy-done.4, bf16[400,4096]{1,0:T(8,128)(2,1)} %get-tuple-element.65, f32[128,4096]{1,0:T(8,128)S(1)} %get-tuple-element.17, bf16[128,4096]{1,0:T(8,128)(2,1)} %get-tuple-element.40), kind=kOutput, calls=%fused_computation | convolution fusion | flops 1289355264 | bytes 13590528 | tf_op jit(solution)/shard_map/dot_general | solution.py:132
  81.1 4.2 %fusion.19 = f32[128,1200]{0,1:T(8,128)S(1)} fusion(f32[128,1200]{0,1:T(8,128)} %fusion, bf16[400,4096]{1,0:T(8,128)(2,1)S(1)} %copy-done.1, bf16[400,4096]{1,0:T(8,128)(2,1)S(1)} %copy-done.2, bf16[400,4096]{1,0:T(8,128)(2,1)S(1)} %copy-done.3, f32[128,4096]{1,0:T(8,128)S(1)} %get-tuple-element.17, bf16[128,4096]{1,0:T(8,128)(2,1)} %get-tuple-element.39), kind=kOutput, calls=%fused_computation.36 | convolution fusion | flops 1289508864 | bytes 14204928 | tf_op jit(solution)/shard_map/dot_general | solution.py:134
  86.2 7.1 %all-to-all-start.1 = ((f32[8,2,128]{2,1,0:T(2,128)}), f32[8,2,128]{2,1,0:T(2,128)S(1)}, u32[]{:S(2)}, u32[]{:S(2)}) async-start(f32[8,2,128]{2,1,0:T(2,128)} %broadcast_in_dim.96), calls=%async_computation.1 | async-start | bytes 16384 | tf_op jit(solution)/shard_map/all_to_all | solution.py:50
  93.3 3.4 %fusion.23 = (bf16[128,4096]{1,0:T(8,128)(2,1)}, bf16[128,4096]{1,0:T(8,128)(2,1)}) fusion(f32[128,4096]{1,0:T(8,128)S(1)} %get-tuple-element.22, bf16[128,4096]{1,0:T(8,128)(2,1)} %get-tuple-element.40, bf16[128,4096]{1,0:T(8,128)(2,1)} %get-tuple-element.39), kind=kLoop, calls=%fused_computation.38 | loop fusion | flops 3145728 | bytes 6291456 | tf_op jit(solution)/shard_map/convert_element_type | solution.py:112
  96.7 3.2 %all-to-all-done.1 = f32[8,2,128]{2,1,0:T(2,128)S(1)} async-done(((f32[8,2,128]{2,1,0:T(2,128)}), f32[8,2,128]{2,1,0:T(2,128)S(1)}, u32[]{:S(2)}, u32[]{:S(2)}) %all-to-all-start.1) | async-done | bytes 8224 | tf_op jit(solution)/shard_map/all_to_all | solution.py:50
  100.6 4.3 %fusion.14 = f32[25,16,12288]{2,1,0:T(8,128)S(1)} fusion(bf16[25,16,128]{2,1,0:T(8,128)(2,1)S(1)} %bitcast.84, bf16[128,4096]{1,0:T(8,128)(2,1)S(1)} %get-tuple-element.23, bf16[128,4096]{1,0:T(8,128)(2,1)} %get-tuple-element.36, bf16[128,4096]{1,0:T(8,128)(2,1)} %get-tuple-element.35), kind=kOutput, calls=%fused_computation.26 | convolution fusion | flops 1267728384 | bytes 22908928 | tf_op jit(solution)/shard_map/dot_general | solution.py:158
  105.0 2.8 %subtract_reduce_fusion = (bf16[16,4096]{1,0:T(8,128)(2,1)S(1)}, bf16[16,4096]{1,0:T(8,128)(2,1)S(1)}, bf16[16,4096]{1,0:T(8,128)(2,1)S(1)}) fusion(f32[25,16,12288]{2,1,0:T(8,128)S(1)} %fusion.14, f32[25,4096]{1,0:T(8,128)S(1)} %copy-done.6, f32[25,4096]{1,0:T(8,128)S(1)} %copy-done.7), kind=kLoop, calls=%fused_computation.18 | loop fusion | flops 14548992 | bytes 20873216 | tf_op jit(solution)/shard_map/reduce_sum | solution.py:167
  107.8 22.1 %all_to_all.15 = bf16[32,8,768]{2,1,0:T(8,128)(2,1)S(1)} all-to-all(bf16[32,8,768]{2,1,0:T(8,128)(2,1)S(1)} %bitcast.81), channel_id=1, replica_groups=mesh['dom'=16,'zz'=8,'cc'=2] {'cc','dom'}, dimensions={0} | all-to-all | bytes 786432 | tf_op jit(solution)/shard_map/all_to_all | solution.py:183
  (75 shorter events, 14.1 us)
Async XLA Ops:
  0.6 23.2 %collective-permute-start = (bf16[16,8192]{1,0:T(8,128)(2,1)}, bf16[16,8192]{1,0:T(8,128)(2,1)S(1)}, u32[]{:S(2)}, u32[]{:S(2)}) collective-permute-start(bf16[16,8192]{1,0:T(8,128)(2,1)} %param.11), channel_id=1, source_target_pairs={{0,2},{2,4},{4,6},{6,8},{8,10},{10,12},{12,14},{14,0},{1,3},{3,5},... | collective-permute-start | bytes 786440 | tf_op jit(solution)/shard_map/ppermute | solution.py:82
  3.2 20.7 %collective-permute-start.1 = (bf16[16,8192]{1,0:T(8,128)(2,1)}, bf16[16,8192]{1,0:T(8,128)(2,1)S(1)}, u32[]{:S(2)}, u32[]{:S(2)}) collective-permute-start(bf16[16,8192]{1,0:T(8,128)(2,1)} %param.11), channel_id=1, source_target_pairs={{0,14},{2,0},{4,2},{6,4},{8,6},{10,8},{12,10},{14,12},{1,15},{3,1}... | collective-permute-start | bytes 786440 | tf_op jit(solution)/shard_map/ppermute | solution.py:83
  11.1 12.4 %all-to-all-start = ((bf16[8,16,256]{2,1,0:T(8,128)(2,1)}), bf16[8,16,256]{2,1,0:T(8,128)(2,1)S(1)}, u32[]{:S(2)}, u32[]{:S(2)}) async-start(bf16[8,16,256]{2,1,0:T(8,128)(2,1)} %broadcast_in_dim.91), calls=%async_computation | async-start | bytes 131072 | tf_op jit(solution)/shard_map/all_to_all | solution.py:50
  23.8 24.3 %copy-start.8 = (bf16[128,256]{0,1:T(8,128)(2,1)}, bf16[128,256]{0,1:T(8,128)(2,1)S(1)}, u32[]{:S(2)}) copy-start(bf16[128,256]{0,1:T(8,128)(2,1)S(1)} %fusion.41) | copy-start | bytes 196612
  26.4 2.7 %copy-start = (f32[25,16,4096]{2,1,0:T(8,128)}, f32[25,16,4096]{2,1,0:T(8,128)S(1)}, u32[]{:S(2)}) copy-start(f32[25,16,4096]{2,1,0:T(8,128)S(1)} %get-tuple-element.38) | copy-start | bytes 19660804
  34.6 13.5 %copy-start.10 = (f32[4096]{0:T(1024)S(1)}, f32[4096]{0:T(1024)}, u32[]{:S(2)}) copy-start(f32[4096]{0:T(1024)} %param.13) | copy-start | bytes 49156
  34.6 13.5 %copy-start.11 = (f32[4096]{0:T(1024)S(1)}, f32[4096]{0:T(1024)}, u32[]{:S(2)}) copy-start(f32[4096]{0:T(1024)} %constant.92.clone) | copy-start | bytes 49156
  41.6 33.5 %copy-start.4 = (bf16[400,4096]{1,0:T(8,128)(2,1)S(1)}, bf16[400,4096]{1,0:T(8,128)(2,1)}, u32[]{:S(2)}) copy-start(bf16[400,4096]{1,0:T(8,128)(2,1)} %get-tuple-element.33) | copy-start | bytes 9830404
  41.6 33.5 %copy-start.5 = (bf16[400,4096]{1,0:T(8,128)(2,1)S(1)}, bf16[400,4096]{1,0:T(8,128)(2,1)}, u32[]{:S(2)}) copy-start(bf16[400,4096]{1,0:T(8,128)(2,1)} %get-tuple-element.34) | copy-start | bytes 9830404
  41.6 6.4 %collective-permute-start.2 = (bf16[16,8192]{1,0:T(8,128)(2,1)S(1)}, bf16[16,8192]{1,0:T(8,128)(2,1)S(1)}, u32[]{:S(2)}, u32[]{:S(2)}) collective-permute-start(bf16[16,8192]{1,0:T(8,128)(2,1)S(1)} %collective-permute-done), channel_id=1, source_target_pairs={{0,2},{2,4},{4,6},{6,8},{8,10},{10,12},{12,14},{14,0},{1,3},{3,5},... | collective-permute-start | bytes 786440 | tf_op jit(solution)/shard_map/ppermute | solution.py:85
  41.9 6.2 %collective-permute-start.3 = (bf16[16,8192]{1,0:T(8,128)(2,1)S(1)}, bf16[16,8192]{1,0:T(8,128)(2,1)S(1)}, u32[]{:S(2)}, u32[]{:S(2)}) collective-permute-start(bf16[16,8192]{1,0:T(8,128)(2,1)S(1)} %collective-permute-done.1), channel_id=1, source_target_pairs={{0,14},{2,0},{4,2},{6,4},{8,6},{10,8},{12,10},{14,12},{1,15},{3,1}... | collective-permute-start | bytes 786440 | tf_op jit(solution)/shard_map/ppermute | solution.py:86
  48.1 11.2 %slice-start = ((bf16[128,256]{0,1:T(8,128)(2,1)}), bf16[128,128]{0,1:T(8,128)(2,1)S(1)}, s32[]{:S(2)}) async-start(bf16[128,256]{0,1:T(8,128)(2,1)} %copy-done.8), calls=%async_computation.3 | async-start | bytes 65536 | tf_op jit(solution)/shard_map/slice | solution.py:95
  55.4 9.2 %collective-permute-start.4 = (bf16[16,8192]{1,0:T(8,128)(2,1)S(1)}, bf16[16,8192]{1,0:T(8,128)(2,1)S(1)}, u32[]{:S(2)}, u32[]{:S(2)}) collective-permute-start(bf16[16,8192]{1,0:T(8,128)(2,1)S(1)} %collective-permute-done.3), channel_id=1, source_target_pairs={{0,14},{2,0},{4,2},{6,4},{8,6},{10,8},{12,10},{14,12},{1,15},{3,1}... | collective-permute-start | bytes 786440 | tf_op jit(solution)/shard_map/ppermute | solution.py:89
  58.2 6.4 %collective-permute-start.5 = (bf16[16,8192]{1,0:T(8,128)(2,1)S(1)}, bf16[16,8192]{1,0:T(8,128)(2,1)S(1)}, u32[]{:S(2)}, u32[]{:S(2)}) collective-permute-start(bf16[16,8192]{1,0:T(8,128)(2,1)S(1)} %collective-permute-done.2), channel_id=1, source_target_pairs={{0,2},{2,4},{4,6},{6,8},{8,10},{10,12},{12,14},{14,0},{1,3},{3,5},... | collective-permute-start | bytes 786440 | tf_op jit(solution)/shard_map/ppermute | solution.py:88
  64.6 7.6 %collective-permute-start.6 = (bf16[16,8192]{1,0:T(8,128)(2,1)S(1)}, bf16[16,8192]{1,0:T(8,128)(2,1)S(1)}, u32[]{:S(2)}, u32[]{:S(2)}) collective-permute-start(bf16[16,8192]{1,0:T(8,128)(2,1)S(1)} %collective-permute-done.5), channel_id=1, source_target_pairs={{0,2},{2,4},{4,6},{6,8},{8,10},{10,12},{12,14},{14,0},{1,3},{3,5},... | collective-permute-start | bytes 786440 | tf_op jit(solution)/shard_map/ppermute | solution.py:90
  75.1 6.0 %copy-start.1 = (bf16[400,4096]{1,0:T(8,128)(2,1)S(1)}, bf16[400,4096]{1,0:T(8,128)(2,1)}, u32[]{:S(2)}) copy-start(bf16[400,4096]{1,0:T(8,128)(2,1)} %get-tuple-element.66) | copy-start | bytes 9830404
  75.1 6.0 %copy-start.2 = (bf16[400,4096]{1,0:T(8,128)(2,1)S(1)}, bf16[400,4096]{1,0:T(8,128)(2,1)}, u32[]{:S(2)}) copy-start(bf16[400,4096]{1,0:T(8,128)(2,1)} %get-tuple-element.67) | copy-start | bytes 9830404
  75.1 6.0 %copy-start.3 = (bf16[400,4096]{1,0:T(8,128)(2,1)S(1)}, bf16[400,4096]{1,0:T(8,128)(2,1)}, u32[]{:S(2)}) copy-start(bf16[400,4096]{1,0:T(8,128)(2,1)} %get-tuple-element.64) | copy-start | bytes 9830404
  85.3 14.6 %copy-start.9 = (bf16[128,256]{0,1:T(8,128)(2,1)S(1)}, bf16[128,256]{0,1:T(8,128)(2,1)}, u32[]{:S(2)}) copy-start(bf16[128,256]{0,1:T(8,128)(2,1)} %copy-done.8) | copy-start | bytes 196612
  86.2 13.7 %all-to-all-start.1 = ((f32[8,2,128]{2,1,0:T(2,128)}), f32[8,2,128]{2,1,0:T(2,128)S(1)}, u32[]{:S(2)}, u32[]{:S(2)}) async-start(f32[8,2,128]{2,1,0:T(2,128)} %broadcast_in_dim.96), calls=%async_computation.1 | async-start | bytes 16384 | tf_op jit(solution)/shard_map/all_to_all | solution.py:50
  100.6 4.4 %copy-start.6 = (f32[25,4096]{1,0:T(8,128)S(1)}, f32[25,4096]{1,0:T(8,128)}, u32[]{:S(2)}) copy-start(f32[25,4096]{1,0:T(8,128)} %constant.91.clone) | copy-start | bytes 1228804
  100.6 4.4 %copy-start.7 = (f32[25,4096]{1,0:T(8,128)S(1)}, f32[25,4096]{1,0:T(8,128)}, u32[]{:S(2)}) copy-start(f32[25,4096]{1,0:T(8,128)} %constant.90.clone) | copy-start | bytes 1228804
